TPU v7x, 32 devices: a whole 2x2x4 slice. The times are simulated.
32 devices in a mesh: block: 8 (over y, x, core), tm: 4 (over z).
Axes of the slice: x: 2, y: 2, z: 4, core: 2. Of those that a mesh axis runs over, the one named last changes fastest.
Arguments:
- traces: bfloat16 [2048, 8, 6, 1024], P('block', 'tm')
- valid: int32 [2048, 8, 6], P('block', 'tm'), may hold values from 0 to 1, as said below
- panel_owner: int32 [4], replicated, may hold values from 0 to 7, as said below
- panel_start: int32 [4], replicated, may hold values from 0 to 252, as said below
Outputs:
- xcorr: float32 [16, 2048, 1024], P('tm', 'block')
Inputs may be any that keep to these rules, and one draw needn't show every extreme that they name: Within one block-tm cell (256 channels by 2 windows by 6 segments) at least an eighth of the segments are valid. `panel_owner`: the panels lie on distinct blocks. `panel_start`: multiples of 4.
All inputs are finite; a program needn't handle non-finite values.
Results may differ from a plain program's by a relative error of at most 0.0051.
Values may be sent and summed in bfloat16 or wider, within the bound.
No kernel may reach another device: no remote copies, remote signals or barrier semaphores. Data moves between devices by JAX's collectives and lax.ppermute only.
A program may use at most 128 MiB of HBM per device.

v0:
```python
import math

import jax
import jax.numpy as jnp
from jax import lax
from jax.sharding import PartitionSpec as P
from jax.experimental import pallas as pl
from jax.experimental.pallas import tpu as pltpu

PP = 4
NP = 4


def spread(value, axis, source):
    kept = jnp.where(lax.axis_index(axis) == source, value, 0).astype(value.dtype)
    return lax.psum(kept, axis)


def forward_table(length):
    sample = jnp.arange(length, dtype=jnp.int32)
    bin_index = jnp.arange(length // 2, dtype=jnp.int32)
    angles = (sample[:, None] * bin_index[None, :] % length).astype(jnp.float32) * (
        2.0 * math.pi / length
    )
    return jnp.concatenate([jnp.cos(angles), -jnp.sin(angles)], axis=1).astype(jnp.bfloat16)


def inverse_table(length, factor):
    bin_index = jnp.arange(length // 2, dtype=jnp.int32)
    lag_index = jnp.arange(length, dtype=jnp.int32)
    angles = (bin_index[:, None] * lag_index[None, :] % length).astype(jnp.float32) * (
        2.0 * math.pi / length
    )
    weight = jnp.where(bin_index == 0, 1.0, 2.0).astype(jnp.float32)[:, None] * factor
    return jnp.concatenate([weight * jnp.cos(angles), -weight * jnp.sin(angles)], axis=0)


def whiten(segment_rows, valid_mask, forward):
    spectrum = jnp.dot(segment_rows, forward, preferred_element_type=jnp.float32)
    energy = jnp.mean(spectrum * spectrum, axis=1, keepdims=True)
    return (spectrum * lax.rsqrt(energy + 1e-06) * valid_mask[:, None].astype(jnp.float32)).astype(
        jnp.bfloat16
    )


def spectra_rows(segment_rows, valid_mask, forward):
    return whiten(segment_rows, valid_mask, forward)


def correlate(left, right):
    bins = left.shape[-1] // 2
    left_both = jnp.concatenate([left[..., :bins], left[..., bins:]], axis=1)
    right_both = jnp.concatenate([right[..., :bins], right[..., bins:]], axis=1)
    right_turn = jnp.concatenate([right[..., bins:], -right[..., :bins]], axis=1)
    real_part = jnp.einsum(
        "jmk,imk->jik", left_both, right_both, preferred_element_type=jnp.float32
    )
    imag_part = jnp.einsum(
        "jmk,imk->jik", left_both, right_turn, preferred_element_type=jnp.float32
    )
    return jnp.concatenate([real_part, imag_part], axis=-1)


def fetch_panel(whitened, panel_root, panel_first):
    candidate = lax.dynamic_slice_in_dim(whitened, panel_first, PP, 0)
    return spread(candidate, "block", panel_root)


def on_device(traces, valid, panel_owner, panel_start):
    channels, windows_here, segments, length = traces.shape
    bins = length // 2
    forward = forward_table(length)
    whitened = spectra_rows(
        traces.reshape(channels * windows_here * segments, length),
        valid.reshape(channels * windows_here * segments),
        forward,
    )
    whitened = whitened.reshape(channels, windows_here, segments, 2 * bins)
    pieces = []
    for panel in range(NP):
        pieces.append(fetch_panel(whitened, panel_owner[panel], panel_start[panel]))
    sources = jnp.concatenate(pieces, axis=0)
    groups = lax.axis_size("tm")
    inverse = inverse_table(length, 1.0 / math.sqrt(bins * windows_here * segments * groups))
    source_count = sources.shape[0]
    own_rows = whitened.reshape(channels, windows_here * segments, 2 * bins)
    source_rows = sources.reshape(source_count, windows_here * segments, 2 * bins)
    stacked = lax.psum_scatter(
        correlate(source_rows, own_rows), "tm", scatter_dimension=0, tiled=True
    )
    return jnp.dot(stacked, inverse, precision=lax.Precision.HIGHEST)


def edge_first(values, groups):
    return lax.ppermute(values, "tm", [(0, 1), (groups - 1, groups - 2)])


def whiten_kernel(rows_ref, forward_ref, mask_ref, out_ref):
    spectrum = jnp.dot(rows_ref[...], forward_ref[...], preferred_element_type=jnp.float32)
    energy = jnp.mean(spectrum * spectrum, axis=1, keepdims=True)
    scaled = spectrum * lax.rsqrt(energy + 1e-06) * mask_ref[...]
    out_ref[...] = scaled.astype(jnp.bfloat16).reshape(out_ref.shape)


def whiten_segments(rows, mask, forward, chunks):
    segments, channels, length = rows.shape
    width = channels // chunks
    return pl.pallas_call(
        whiten_kernel,
        grid=(segments,),
        in_specs=[
            pl.BlockSpec((None, channels, length), lambda m: (m, 0, 0)),
            pl.BlockSpec((length, length), lambda m: (0, 0)),
            pl.BlockSpec((None, channels, 1), lambda m: (m, 0, 0)),
        ],
        out_specs=pl.BlockSpec((chunks, None, width, length), lambda m: (0, m, 0, 0)),
        out_shape=jax.ShapeDtypeStruct((chunks, segments, width, length), jnp.bfloat16),
    )(rows, forward, mask)


LANES = 128
ROWS = 8


def cross_kernel(own_ref, edge_ref, own_src_ref, edge_src_ref, out_ref):
    segments = own_ref.shape[0]
    sources = own_src_ref.shape[1]
    bins = own_ref.shape[-1] // 2
    for half in range(own_ref.shape[1] // ROWS):
        rows = pl.ds(half * ROWS, ROWS)
        for tile in range(bins // LANES):
            re_lanes = pl.ds(tile * LANES, LANES)
            im_lanes = pl.ds(bins + tile * LANES, LANES)

            def step(m, acc, data_ref, src_ref):
                wr = data_ref[m, rows, re_lanes].astype(jnp.float32)
                wi = data_ref[m, rows, im_lanes].astype(jnp.float32)
                out = []
                for j in range(sources):
                    sr = src_ref[m, j, :, re_lanes]
                    si = src_ref[m, j, :, im_lanes]
                    out.append(acc[2 * j] + (wr * sr + wi * si))
                    out.append(acc[2 * j + 1] + (wi * sr - wr * si))
                return tuple(out)

            acc = tuple(jnp.zeros((ROWS, LANES), jnp.float32) for _ in range(2 * sources))
            acc = lax.fori_loop(0, segments, lambda m, a: step(m, a, own_ref, own_src_ref), acc)
            acc = lax.fori_loop(0, segments, lambda m, a: step(m, a, edge_ref, edge_src_ref), acc)
            for j in range(sources):
                out_ref[j, rows, re_lanes] = acc[2 * j]
                out_ref[j, rows, im_lanes] = acc[2 * j + 1]


def cross_chunk(own, edge, own_src, edge_src):
    segments, width, length = own.shape
    sources = own_src.shape[1]
    step_rows = 2 * ROWS
    return pl.pallas_call(
        cross_kernel,
        grid=(width // step_rows,),
        in_specs=[
            pl.BlockSpec((segments, step_rows, length), lambda i: (0, i, 0)),
            pl.BlockSpec((segments, step_rows, length), lambda i: (0, i, 0)),
            pl.BlockSpec((segments, sources, ROWS, length), lambda i: (0, 0, 0, 0)),
            pl.BlockSpec((segments, sources, ROWS, length), lambda i: (0, 0, 0, 0)),
        ],
        out_specs=pl.BlockSpec((sources, step_rows, length), lambda i: (0, i, 0)),
        out_shape=jax.ShapeDtypeStruct((sources, width, length), jnp.float32),
    )(own, edge, own_src, edge_src)


def butterfly_sum(values, axis):
    count = lax.axis_size(axis)
    step = 1
    while step < count:
        values = values + lax.ppermute(values, axis, [(b, b ^ step) for b in range(count)])
        step *= 2
    return values


def widen(values, length):
    segments, count = values.shape[0], values.shape[1]
    return jnp.broadcast_to(values.astype(jnp.float32)[:, :, None, :], (segments, count, ROWS, length))


def on_line(traces, valid, panel_owner, panel_start):
    channels, windows_here, segments, length = traces.shape
    bins = length // 2
    groups = lax.axis_size("tm")
    place = lax.axis_index("tm")
    chunks = 8
    width = channels // chunks
    seg_count = windows_here * segments
    forward = forward_table(length)
    rows = traces.reshape(channels, seg_count, length).transpose(1, 0, 2)
    mask = valid.reshape(channels, seg_count).transpose(1, 0).astype(jnp.float32)[:, :, None]
    whitened = whiten_segments(rows, mask, forward, chunks)
    block_place = lax.axis_index("block")
    pieces = []
    for panel in range(NP):
        first = panel_start[panel]
        chunk_of = first // width
        candidate = lax.dynamic_slice_in_dim(
            lax.dynamic_index_in_dim(whitened, chunk_of, 0, keepdims=False), first - chunk_of * width, PP, 1
        )
        pieces.append(jnp.where(block_place == panel_owner[panel], candidate, 0).astype(candidate.dtype))
    sources = butterfly_sum(jnp.concatenate(pieces, axis=1), "block")
    source_count = sources.shape[1]
    per_group = source_count // groups
    half = source_count // 2
    first_half = place < groups // 2
    turned = jnp.concatenate(
        [sources[:, source_count - per_group:], sources[:, half:source_count - per_group]], axis=1
    )
    far = jnp.where(first_half, turned, sources[:, :half])
    near = jnp.where(first_half, sources[:, :half], turned)
    inverse = inverse_table(length, 1.0 / math.sqrt(bins * seg_count * groups))
    is_edge = jnp.logical_or(place == 0, place == groups - 1)
    edge_chunks = [edge_first(whitened[0], groups)]
    pair = jnp.concatenate([far, near], axis=1)
    pair, _ = lax.optimization_barrier((pair, edge_chunks[0]))
    edge_pair = edge_first(pair, groups)
    far_wide, edge_far_wide = widen(far, length), widen(edge_pair[:, :half], length)
    near_wide, edge_near_wide = widen(near, length), widen(edge_pair[:, half:], length)
    previous = edge_pair
    for chunk in range(1, chunks):
        own, _ = lax.optimization_barrier((whitened[chunk], previous))
        previous = edge_first(own, groups)
        edge_chunks.append(previous)
    outs = []
    last_sent = None
    for chunk in range(chunks):
        own = whitened[chunk]
        edge_rows = edge_chunks[chunk]
        far_part = cross_chunk(own, edge_rows, far_wide, edge_far_wide)
        if last_sent is not None:
            far_part, _ = lax.optimization_barrier((far_part, last_sent))
        got = lax.ppermute(far_part, "tm", [(1, 2), (2, 1)])
        last_sent = got
        total = cross_chunk(own, edge_rows, near_wide, edge_near_wide) + got
        back = lax.ppermute(total[:per_group], "tm", [(1, 0), (2, 3)])
        final = jnp.where(is_edge, back, total[per_group:])
        outs.append(jnp.dot(final, inverse, precision=lax.Precision.HIGHEST))
    return jnp.concatenate(outs, axis=1)


def solution(mesh):
    in_specs = (P("block", "tm", None, None), P("block", "tm", None), P(), P())
    out_specs = P("tm", "block", None)
    body = on_line if mesh.shape["tm"] == 4 else on_device
    return jax.shard_map(
        body, mesh=mesh, in_specs=in_specs, out_specs=out_specs, check_vma=False
    )
```

profile of v0, /device:TPU:0, one launch (start us, length us, event | category | flops | bytes accessed | tf_op | source)
XLA Modules:
  0.0 475.9 jit_solution(4380770061334723515)
XLA Ops:
  14.5 8.5 %negate_convert_fusion = (bf16[1024,512]{1,0:T(8,128)(2,1)S(1)}, bf16[1024,512]{1,0:T(8,128)(2,1)S(1)}) fusion(), kind=kLoop, calls=%fused_computation.18 | loop fusion | flops 8912896 | bytes 2097152 | tf_op jit(solution)/shard_map/convert.1
  26.4 7.6 %copy.7 = bf16[256,2,6,1024]{3,0,2,1:T(8,128)(2,1)} copy(bf16[256,2,6,1024]{3,1,2,0:T(2,128)(2,1)} %param.4) | data formatting | bytes 12582912 | tf_op args[0]
  37.3 15.3 %shard_map.46 = bf16[8,12,32,1024]{3,2,1,0:T(8,128)(2,1)} custom-call(bf16[12,256,1024]{2,1,0:T(8,128)(2,1)} %bitcast.50, bf16[1024,1024]{1,0:T(8,128)(2,1)} %pad_maximum_fusion.forward_ref, f32[12,256,1]{2,1,0:T(8,128)} %copy.9.mask_ref), custom_call_target="tpu_custom_call" | custom-call | tf_op jit(solution)/shard_map/pallas_call | solution.py:108
  56.6 2.9 collective-permute-start.2
  59.6 9.4 %collective-permute-done.2 = bf16[12,16,1024]{2,1,0:T(8,128)(2,1)S(1)} collective-permute-done((bf16[12,16,1024]{2,1,0:T(8,128)(2,1)S(1)}, bf16[12,16,1024]{2,1,0:T(8,128)(2,1)S(1)}, u32[]{:S(2)}, u32[]{:S(2)}) %collective-permute-start.2) | collective-permute-done | bytes 393248 | tf_op jit(solution)/shard_map/ppermute | solution.py:176
  71.0 5.1 %slice_bitcast_fusion = (bf16[12,32,1024]{2,1,0:T(8,128)(2,1)S(1)}, bf16[12,32,1024]{2,1,0:T(8,128)(2,1)S(1)}, bf16[12,32,1024]{2,1,0:T(8,128)(2,1)S(1)}, bf16[1...) fusion(bf16[8,12,32,1024]{3,2,1,0:T(8,128)(2,1)} %shard_map.46), kind=kLoop, calls=%fused_computation.32 | loop fusion | bytes 12582912 | tf_op jit(solution)/shard_map/squeeze | solution.py:233
  76.1 4.4 collective-permute-start
  81.9 14.0 %collective-permute-done.edge_ref = bf16[12,32,1024]{2,1,0:T(8,128)(2,1)} collective-permute-done((bf16[12,32,1024]{2,1,0:T(8,128)(2,1)}, bf16[12,32,1024]{2,1,0:T(8,128)(2,1)}, u32[]{:S(2)}, u32[]{:S(2)}) %collective-permute-start) | collective-permute-done | bytes 786464 | tf_op jit(solution)/shard_map/ppermute | solution.py:95
  95.9 4.4 collective-permute-start.4
  100.3 6.6 %collective-permute-done.4 = bf16[12,16,1024]{2,1,0:T(8,128)(2,1)S(1)} collective-permute-done((bf16[12,16,1024]{2,1,0:T(8,128)(2,1)S(1)}, bf16[12,16,1024]{2,1,0:T(8,128)(2,1)S(1)}, u32[]{:S(2)}, u32[]{:S(2)}) %collective-permute-start.4) | collective-permute-done | bytes 393248 | tf_op jit(solution)/shard_map/ppermute | solution.py:95
  111.9 9.8 %shard_map.48 = f32[8,32,1024]{2,1,0:T(8,128)} custom-call(bf16[12,32,1024]{2,1,0:T(8,128)(2,1)} %get-tuple-element.42.own_ref, bf16[12,32,1024]{2,1,0:T(8,128)(2,1)} %collective-permute-done.edge_ref, f32[12,8,8,1024]{3,2,1,0:T(8,128)} %broadcast_in_dim.51.own_src_ref, f32[12,8,8,1024]{3,2,1,0:T(8,128)} %broadcast_in_dim.52.edge_src_ref), custom_call_target="tpu_custom_call" | custom-call | tf_op jit(solution)/shard_map/pallas_call | solution.py:158
  123.4 7.1 %collective-permute-start.7 = (bf16[12,32,1024]{2,1,0:T(8,128)(2,1)}, bf16[12,32,1024]{2,1,0:T(8,128)(2,1)}, u32[]{:S(2)}, u32[]{:S(2)}) collective-permute-start(bf16[12,32,1024]{2,1,0:T(8,128)(2,1)} %get-tuple-element.21.own_ref), channel_id=1, source_target_pairs={{0,1},{3,2},{4,5},{7,6},{8,9},{11,10},{12,13},{15,14},{16,17},{19,... | collective-permute-start | bytes 2359304 | tf_op jit(solution)/shard_map/ppermute | solution.py:95
  130.5 13.3 %collective-permute-done.7.edge_ref = bf16[12,32,1024]{2,1,0:T(8,128)(2,1)} collective-permute-done((bf16[12,32,1024]{2,1,0:T(8,128)(2,1)}, bf16[12,32,1024]{2,1,0:T(8,128)(2,1)}, u32[]{:S(2)}, u32[]{:S(2)}) %collective-permute-start.7) | collective-permute-done | bytes 786464 | tf_op jit(solution)/shard_map/ppermute | solution.py:95
  143.8 9.8 %shard_map.50 = f32[8,32,1024]{2,1,0:T(8,128)} custom-call(bf16[12,32,1024]{2,1,0:T(8,128)(2,1)} %get-tuple-element.21.own_ref, bf16[12,32,1024]{2,1,0:T(8,128)(2,1)} %collective-permute-done.7.edge_ref, f32[12,8,8,1024]{3,2,1,0:T(8,128)} %broadcast_in_dim.51.own_src_ref, f32[12,8,8,1024]{3,2,1,0:T(8,128)} %broadcast_in_dim.52.edge_src_ref), custom_call_target="tpu_custom_call" | custom-call | tf_op jit(solution)/shard_map/pallas_call | solution.py:158
  155.3 6.0 %collective-permute-start.10 = (bf16[12,32,1024]{2,1,0:T(8,128)(2,1)}, bf16[12,32,1024]{2,1,0:T(8,128)(2,1)}, u32[]{:S(2)}, u32[]{:S(2)}) collective-permute-start(bf16[12,32,1024]{2,1,0:T(8,128)(2,1)} %get-tuple-element.23.own_ref), channel_id=1, source_target_pairs={{0,1},{3,2},{4,5},{7,6},{8,9},{11,10},{12,13},{15,14},{16,17},{19,... | collective-permute-start | bytes 2359304 | tf_op jit(solution)/shard_map/ppermute | solution.py:95
  161.3 12.0 %collective-permute-done.10.edge_ref = bf16[12,32,1024]{2,1,0:T(8,128)(2,1)} collective-permute-done((bf16[12,32,1024]{2,1,0:T(8,128)(2,1)}, bf16[12,32,1024]{2,1,0:T(8,128)(2,1)}, u32[]{:S(2)}, u32[]{:S(2)}) %collective-permute-start.10) | collective-permute-done | bytes 786464 | tf_op jit(solution)/shard_map/ppermute | solution.py:95
  173.4 9.8 %shard_map.52 = f32[8,32,1024]{2,1,0:T(8,128)} custom-call(bf16[12,32,1024]{2,1,0:T(8,128)(2,1)} %get-tuple-element.23.own_ref, bf16[12,32,1024]{2,1,0:T(8,128)(2,1)} %collective-permute-done.10.edge_ref, f32[12,8,8,1024]{3,2,1,0:T(8,128)} %broadcast_in_dim.51.own_src_ref, f32[12,8,8,1024]{3,2,1,0:T(8,128)} %broadcast_in_dim.52.edge_src_ref), custom_call_target="tpu_custom_call" | custom-call | tf_op jit(solution)/shard_map/pallas_call | solution.py:158
  184.8 7.1 %collective-permute-start.13 = (bf16[12,32,1024]{2,1,0:T(8,128)(2,1)}, bf16[12,32,1024]{2,1,0:T(8,128)(2,1)}, u32[]{:S(2)}, u32[]{:S(2)}) collective-permute-start(bf16[12,32,1024]{2,1,0:T(8,128)(2,1)} %get-tuple-element.25.own_ref), channel_id=1, source_target_pairs={{0,1},{3,2},{4,5},{7,6},{8,9},{11,10},{12,13},{15,14},{16,17},{19,... | collective-permute-start | bytes 2359304 | tf_op jit(solution)/shard_map/ppermute | solution.py:95
  192.0 10.9 %collective-permute-done.13.edge_ref = bf16[12,32,1024]{2,1,0:T(8,128)(2,1)} collective-permute-done((bf16[12,32,1024]{2,1,0:T(8,128)(2,1)}, bf16[12,32,1024]{2,1,0:T(8,128)(2,1)}, u32[]{:S(2)}, u32[]{:S(2)}) %collective-permute-start.13) | collective-permute-done | bytes 786464 | tf_op jit(solution)/shard_map/ppermute | solution.py:95
  202.8 9.8 %shard_map.54 = f32[8,32,1024]{2,1,0:T(8,128)} custom-call(bf16[12,32,1024]{2,1,0:T(8,128)(2,1)} %get-tuple-element.25.own_ref, bf16[12,32,1024]{2,1,0:T(8,128)(2,1)} %collective-permute-done.13.edge_ref, f32[12,8,8,1024]{3,2,1,0:T(8,128)} %broadcast_in_dim.51.own_src_ref, f32[12,8,8,1024]{3,2,1,0:T(8,128)} %broadcast_in_dim.52.edge_src_ref), custom_call_target="tpu_custom_call" | custom-call | tf_op jit(solution)/shard_map/pallas_call | solution.py:158
  214.3 6.0 %collective-permute-start.16 = (bf16[12,32,1024]{2,1,0:T(8,128)(2,1)S(1)}, bf16[12,32,1024]{2,1,0:T(8,128)(2,1)}, u32[]{:S(2)}, u32[]{:S(2)}) collective-permute-start(bf16[12,32,1024]{2,1,0:T(8,128)(2,1)S(1)} %get-tuple-element.27.own_ref), channel_id=1, source_target_pairs={{0,1},{3,2},{4,5},{7,6},{8,9},{11,10},{12,13},{15,14},{16,17},{19,... | collective-permute-start | bytes 2359304 | tf_op jit(solution)/shard_map/ppermute | solution.py:95
  220.3 9.4 %collective-permute-done.16.edge_ref = bf16[12,32,1024]{2,1,0:T(8,128)(2,1)} collective-permute-done((bf16[12,32,1024]{2,1,0:T(8,128)(2,1)S(1)}, bf16[12,32,1024]{2,1,0:T(8,128)(2,1)}, u32[]{:S(2)}, u32[]{:S(2)}) %collective-permute-start.16) | collective-permute-done | bytes 786464 | tf_op jit(solution)/shard_map/ppermute | solution.py:95
  229.7 9.8 %shard_map.56 = f32[8,32,1024]{2,1,0:T(8,128)} custom-call(bf16[12,32,1024]{2,1,0:T(8,128)(2,1)} %copy-done.7, bf16[12,32,1024]{2,1,0:T(8,128)(2,1)} %collective-permute-done.16.edge_ref, f32[12,8,8,1024]{3,2,1,0:T(8,128)} %broadcast_in_dim.51.own_src_ref, f32[12,8,8,1024]{3,2,1,0:T(8,128)} %broadcast_in_dim.52.edge_src_ref), custom_call_target="tpu_custom_call" | custom-call | tf_op jit(solution)/shard_map/pallas_call | solution.py:158
  241.2 6.3 %collective-permute-start.19 = (bf16[12,32,1024]{2,1,0:T(8,128)(2,1)S(1)}, bf16[12,32,1024]{2,1,0:T(8,128)(2,1)S(1)}, u32[]{:S(2)}, u32[]{:S(2)}) collective-permute-start(bf16[12,32,1024]{2,1,0:T(8,128)(2,1)S(1)} %get-tuple-element.29.own_ref), channel_id=1, source_target_pairs={{0,1},{3,2},{4,5},{7,6},{8,9},{11,10},{12,13},{15,14},{16,17},{19,... | collective-permute-start | bytes 2359304 | tf_op jit(solution)/shard_map/ppermute | solution.py:95
  247.5 9.4 %collective-permute-done.19.edge_ref = bf16[12,32,1024]{2,1,0:T(8,128)(2,1)S(1)} collective-permute-done((bf16[12,32,1024]{2,1,0:T(8,128)(2,1)S(1)}, bf16[12,32,1024]{2,1,0:T(8,128)(2,1)S(1)}, u32[]{:S(2)}, u32[]{:S(2)}) %collective-permute-start.19) | collective-permute-done | bytes 786464 | tf_op jit(solution)/shard_map/ppermute | solution.py:95
  257.9 9.8 %shard_map.58 = f32[8,32,1024]{2,1,0:T(8,128)} custom-call(bf16[12,32,1024]{2,1,0:T(8,128)(2,1)} %copy-done.6, bf16[12,32,1024]{2,1,0:T(8,128)(2,1)} %copy-done.20, f32[12,8,8,1024]{3,2,1,0:T(8,128)} %broadcast_in_dim.51.own_src_ref, f32[12,8,8,1024]{3,2,1,0:T(8,128)} %broadcast_in_dim.52.edge_src_ref), custom_call_target="tpu_custom_call" | custom-call | tf_op jit(solution)/shard_map/pallas_call | solution.py:158
  269.3 5.3 %collective-permute-start.22 = (bf16[12,32,1024]{2,1,0:T(8,128)(2,1)S(1)}, bf16[12,32,1024]{2,1,0:T(8,128)(2,1)S(1)}, u32[]{:S(2)}, u32[]{:S(2)}) collective-permute-start(bf16[12,32,1024]{2,1,0:T(8,128)(2,1)S(1)} %get-tuple-element.31.own_ref), channel_id=1, source_target_pairs={{0,1},{3,2},{4,5},{7,6},{8,9},{11,10},{12,13},{15,14},{16,17},{19,... | collective-permute-start | bytes 2359304 | tf_op jit(solution)/shard_map/ppermute | solution.py:95
  274.6 9.4 %collective-permute-done.22.edge_ref = bf16[12,32,1024]{2,1,0:T(8,128)(2,1)S(1)} collective-permute-done((bf16[12,32,1024]{2,1,0:T(8,128)(2,1)S(1)}, bf16[12,32,1024]{2,1,0:T(8,128)(2,1)S(1)}, u32[]{:S(2)}, u32[]{:S(2)}) %collective-permute-start.22) | collective-permute-done | bytes 786464 | tf_op jit(solution)/shard_map/ppermute | solution.py:95
  285.0 9.8 %shard_map.60 = f32[8,32,1024]{2,1,0:T(8,128)} custom-call(bf16[12,32,1024]{2,1,0:T(8,128)(2,1)} %copy-done.5, bf16[12,32,1024]{2,1,0:T(8,128)(2,1)} %copy-done.21, f32[12,8,8,1024]{3,2,1,0:T(8,128)} %broadcast_in_dim.51.own_src_ref, f32[12,8,8,1024]{3,2,1,0:T(8,128)} %broadcast_in_dim.52.edge_src_ref), custom_call_target="tpu_custom_call" | custom-call | tf_op jit(solution)/shard_map/pallas_call | solution.py:158
  300.7 9.8 %shard_map.47 = f32[8,32,1024]{2,1,0:T(8,128)} custom-call(bf16[12,32,1024]{2,1,0:T(8,128)(2,1)} %get-tuple-element.42.own_ref, bf16[12,32,1024]{2,1,0:T(8,128)(2,1)} %collective-permute-done.edge_ref, f32[12,8,8,1024]{3,2,1,0:T(8,128)} %broadcast_in_dim.27.own_src_ref, f32[12,8,8,1024]{3,2,1,0:T(8,128)} %broadcast_in_dim.50.edge_src_ref), custom_call_target="tpu_custom_call" | custom-call | tf_op jit(solution)/shard_map/pallas_call | solution.py:158
  314.4 7.2 %collective-permute-start.25 = (bf16[12,32,1024]{2,1,0:T(8,128)(2,1)S(1)}, bf16[12,32,1024]{2,1,0:T(8,128)(2,1)}, u32[]{:S(2)}, u32[]{:S(2)}) collective-permute-start(bf16[12,32,1024]{2,1,0:T(8,128)(2,1)S(1)} %get-tuple-element.33.own_ref), channel_id=1, source_target_pairs={{0,1},{3,2},{4,5},{7,6},{8,9},{11,10},{12,13},{15,14},{16,17},{19,... | collective-permute-start | bytes 2359304 | tf_op jit(solution)/shard_map/ppermute | solution.py:95
  321.6 9.8 %shard_map.49 = f32[8,32,1024]{2,1,0:T(8,128)} custom-call(bf16[12,32,1024]{2,1,0:T(8,128)(2,1)} %get-tuple-element.21.own_ref, bf16[12,32,1024]{2,1,0:T(8,128)(2,1)} %collective-permute-done.7.edge_ref, f32[12,8,8,1024]{3,2,1,0:T(8,128)} %broadcast_in_dim.27.own_src_ref, f32[12,8,8,1024]{3,2,1,0:T(8,128)} %broadcast_in_dim.50.edge_src_ref), custom_call_target="tpu_custom_call" | custom-call | tf_op jit(solution)/shard_map/pallas_call | solution.py:158
  335.5 9.2 %sine_multiply_fusion = (f32[512,1024]{1,0:T(8,128)S(1)}, f32[512,1024]{1,0:T(8,128)}) fusion(f32[512]{0:T(512)S(1)} %fusion.20, f32[512]{0:T(512)S(1)} %select_multiply_fusion), kind=kLoop, calls=%fused_computation.14 | loop fusion | flops 8388608 | bytes 4198400 | tf_op jit(solution)/shard_map/mul | solution.py:35
  344.8 9.8 %shard_map.51 = f32[8,32,1024]{2,1,0:T(8,128)} custom-call(bf16[12,32,1024]{2,1,0:T(8,128)(2,1)} %get-tuple-element.23.own_ref, bf16[12,32,1024]{2,1,0:T(8,128)(2,1)} %collective-permute-done.10.edge_ref, f32[12,8,8,1024]{3,2,1,0:T(8,128)} %broadcast_in_dim.27.own_src_ref, f32[12,8,8,1024]{3,2,1,0:T(8,128)} %broadcast_in_dim.50.edge_src_ref), custom_call_target="tpu_custom_call" | custom-call | tf_op jit(solution)/shard_map/pallas_call | solution.py:158
  359.7 3.2 convolution_dynamic-update-slice_fusion.7
  362.9 9.8 %shard_map.53 = f32[8,32,1024]{2,1,0:T(8,128)} custom-call(bf16[12,32,1024]{2,1,0:T(8,128)(2,1)} %get-tuple-element.25.own_ref, bf16[12,32,1024]{2,1,0:T(8,128)(2,1)} %collective-permute-done.13.edge_ref, f32[12,8,8,1024]{3,2,1,0:T(8,128)} %broadcast_in_dim.27.own_src_ref, f32[12,8,8,1024]{3,2,1,0:T(8,128)} %broadcast_in_dim.50.edge_src_ref), custom_call_target="tpu_custom_call" | custom-call | tf_op jit(solution)/shard_map/pallas_call | solution.py:158
  377.5 9.8 %shard_map.62 = f32[8,32,1024]{2,1,0:T(8,128)} custom-call(bf16[12,32,1024]{2,1,0:T(8,128)(2,1)} %copy-done.4, bf16[12,32,1024]{2,1,0:T(8,128)(2,1)} %collective-permute-done.25.edge_ref, f32[12,8,8,1024]{3,2,1,0:T(8,128)} %broadcast_in_dim.51.own_src_ref, f32[12,8,8,1024]{3,2,1,0:T(8,128)} %broadcast_in_dim.52.edge_src_ref), custom_call_target="tpu_custom_call" | custom-call | tf_op jit(solution)/shard_map/pallas_call | solution.py:158
  389.0 5.1 %convolution_dynamic-update-slice_fusion.6 = f32[4,256,1024]{2,1,0:T(8,128)} fusion(f32[4,256,1024]{2,1,0:T(8,128)} %convolution_dynamic-update-slice_fusion.7, f32[4,32,1024]{2,1,0:T(8,128)} %collective-permute-done.9, f32[8,32,1024]{2,1,0:T(8,128)} %copy-done.13, pred[]{:T(512)S(6)} %or.3, f32[512,1024]{1,0:T(8,128)S(1)} %get-tuple-element.63, ...), kind=kOutput, calls=%fused_computation.30 | convolution fusion | flops 1611792384 | bytes 5767169 | tf_op jit(solution)/shard_map/dot_general | solution.py:243
  394.1 9.8 %shard_map.55 = f32[8,32,1024]{2,1,0:T(8,128)} custom-call(bf16[12,32,1024]{2,1,0:T(8,128)(2,1)} %copy-done.7, bf16[12,32,1024]{2,1,0:T(8,128)(2,1)} %collective-permute-done.16.edge_ref, f32[12,8,8,1024]{3,2,1,0:T(8,128)} %broadcast_in_dim.27.own_src_ref, f32[12,8,8,1024]{3,2,1,0:T(8,128)} %broadcast_in_dim.50.edge_src_ref), custom_call_target="tpu_custom_call" | custom-call | tf_op jit(solution)/shard_map/pallas_call | solution.py:158
  409.2 4.2 convolution_dynamic-update-slice_fusion.5
  413.4 9.8 %shard_map.57 = f32[8,32,1024]{2,1,0:T(8,128)} custom-call(bf16[12,32,1024]{2,1,0:T(8,128)(2,1)} %copy-done.6, bf16[12,32,1024]{2,1,0:T(8,128)(2,1)} %copy-done.20, f32[12,8,8,1024]{3,2,1,0:T(8,128)} %broadcast_in_dim.27.own_src_ref, f32[12,8,8,1024]{3,2,1,0:T(8,128)} %broadcast_in_dim.50.edge_src_ref), custom_call_target="tpu_custom_call" | custom-call | tf_op jit(solution)/shard_map/pallas_call | solution.py:158
  423.2 9.8 %shard_map.59 = f32[8,32,1024]{2,1,0:T(8,128)} custom-call(bf16[12,32,1024]{2,1,0:T(8,128)(2,1)} %copy-done.5, bf16[12,32,1024]{2,1,0:T(8,128)(2,1)} %copy-done.21, f32[12,8,8,1024]{3,2,1,0:T(8,128)} %broadcast_in_dim.27.own_src_ref, f32[12,8,8,1024]{3,2,1,0:T(8,128)} %broadcast_in_dim.50.edge_src_ref), custom_call_target="tpu_custom_call" | custom-call | tf_op jit(solution)/shard_map/pallas_call | solution.py:158
  438.1 3.2 convolution_dynamic-update-slice_fusion.4
  441.3 9.8 %shard_map.61 = f32[8,32,1024]{2,1,0:T(8,128)} custom-call(bf16[12,32,1024]{2,1,0:T(8,128)(2,1)} %copy-done.4, bf16[12,32,1024]{2,1,0:T(8,128)(2,1)} %collective-permute-done.25.edge_ref, f32[12,8,8,1024]{3,2,1,0:T(8,128)} %broadcast_in_dim.27.own_src_ref, f32[12,8,8,1024]{3,2,1,0:T(8,128)} %broadcast_in_dim.50.edge_src_ref), custom_call_target="tpu_custom_call" | custom-call | tf_op jit(solution)/shard_map/pallas_call | solution.py:158
  454.5 3.2 convolution_dynamic-update-slice_fusion.3
  460.8 4.2 convolution_dynamic-update-slice_fusion.2
  466.4 3.2 convolution_dynamic-update-slice_fusion.1
  472.3 3.2 convolution_dynamic-update-slice_fusion
  (125 shorter events, 75.4 us)
Async XLA Ops:
  0.0 23.1 %copy-start.24 = (s32[4]{0:T(128)S(1)}, s32[4]{0:T(128)}, u32[]{:S(2)}) copy-start(s32[4]{0:T(128)} %param.6) | copy-start | bytes 52
  26.4 7.6 %copy-start.23 = (s32[256,2,6]{0,1,2:T(2,128)S(1)}, s32[256,2,6]{0,1,2:T(2,128)}, u32[]{:S(2)}) copy-start(s32[256,2,6]{0,1,2:T(2,128)} %param.5) | copy-start | bytes 36868
  54.5 1.9 collective-permute-start.1
  56.6 12.3 %collective-permute-start.2 = (bf16[12,16,1024]{2,1,0:T(8,128)(2,1)S(1)}, bf16[12,16,1024]{2,1,0:T(8,128)(2,1)S(1)}, u32[]{:S(2)}, u32[]{:S(2)}) collective-permute-start(bf16[12,16,1024]{2,1,0:T(8,128)(2,1)S(1)} %fusion.21), channel_id=1, source_target_pairs={{0,8},{4,12},{8,0},{12,4},{16,24},{20,28},{24,16},{28,20},{1,9},{5... | collective-permute-start | bytes 1179656 | tf_op jit(solution)/shard_map/ppermute | solution.py:176
  69.1 11.4 %collective-permute-start.3 = (bf16[12,16,1024]{2,1,0:T(8,128)(2,1)S(1)}, bf16[12,16,1024]{2,1,0:T(8,128)(2,1)}, u32[]{:S(2)}, u32[]{:S(2)}) collective-permute-start(bf16[12,16,1024]{2,1,0:T(8,128)(2,1)S(1)} %add.104), channel_id=1, source_target_pairs={{0,16},{4,20},{8,24},{12,28},{16,0},{20,4},{24,8},{28,12},{1,17},{... | collective-permute-start | bytes 1179656 | tf_op jit(solution)/shard_map/ppermute | solution.py:176
  76.1 138.2 %copy-start.7 = (bf16[12,32,1024]{2,1,0:T(8,128)(2,1)}, bf16[12,32,1024]{2,1,0:T(8,128)(2,1)S(1)}, u32[]{:S(2)}) copy-start(bf16[12,32,1024]{2,1,0:T(8,128)(2,1)S(1)} %get-tuple-element.27.own_ref) | copy-start | bytes 2359300
  76.1 165.1 %copy-start.6 = (bf16[12,32,1024]{2,1,0:T(8,128)(2,1)}, bf16[12,32,1024]{2,1,0:T(8,128)(2,1)S(1)}, u32[]{:S(2)}) copy-start(bf16[12,32,1024]{2,1,0:T(8,128)(2,1)S(1)} %get-tuple-element.29.own_ref) | copy-start | bytes 2359300
  76.1 193.2 %copy-start.5 = (bf16[12,32,1024]{2,1,0:T(8,128)(2,1)}, bf16[12,32,1024]{2,1,0:T(8,128)(2,1)S(1)}, u32[]{:S(2)}) copy-start(bf16[12,32,1024]{2,1,0:T(8,128)(2,1)S(1)} %get-tuple-element.31.own_ref) | copy-start | bytes 2359300
  76.1 238.3 %copy-start.4 = (bf16[12,32,1024]{2,1,0:T(8,128)(2,1)}, bf16[12,32,1024]{2,1,0:T(8,128)(2,1)S(1)}, u32[]{:S(2)}) copy-start(bf16[12,32,1024]{2,1,0:T(8,128)(2,1)S(1)} %get-tuple-element.33.own_ref) | copy-start | bytes 2359300
  76.1 19.8 %collective-permute-start = (bf16[12,32,1024]{2,1,0:T(8,128)(2,1)}, bf16[12,32,1024]{2,1,0:T(8,128)(2,1)}, u32[]{:S(2)}, u32[]{:S(2)}) collective-permute-start(bf16[12,32,1024]{2,1,0:T(8,128)(2,1)} %get-tuple-element.42.own_ref), channel_id=1, source_target_pairs={{0,1},{3,2},{4,5},{7,6},{8,9},{11,10},{12,13},{15,14},{16,17},{19,... | collective-permute-start | bytes 2359304 | tf_op jit(solution)/shard_map/ppermute | solution.py:95
  95.9 11.0 %collective-permute-start.4 = (bf16[12,16,1024]{2,1,0:T(8,128)(2,1)S(1)}, bf16[12,16,1024]{2,1,0:T(8,128)(2,1)S(1)}, u32[]{:S(2)}, u32[]{:S(2)}) collective-permute-start(bf16[12,16,1024]{2,1,0:T(8,128)(2,1)S(1)} %pad_maximum_fusion.2), channel_id=1, source_target_pairs={{0,1},{3,2},{4,5},{7,6},{8,9},{11,10},{12,13},{15,14},{16,17},{19,... | collective-permute-start | bytes 1179656 | tf_op jit(solution)/shard_map/ppermute | solution.py:95
  121.8 31.9 %collective-permute-start.5 = (f32[8,32,1024]{2,1,0:T(8,128)}, f32[8,32,1024]{2,1,0:T(8,128)}, u32[]{:S(2)}, u32[]{:S(2)}) collective-permute-start(f32[8,32,1024]{2,1,0:T(8,128)} %shard_map.48), channel_id=1, source_target_pairs={{1,2},{2,1},{5,6},{6,5},{9,10},{10,9},{13,14},{14,13},{17,18},{18,... | collective-permute-start | bytes 3145736 | tf_op jit(solution)/shard_map/ppermute | solution.py:238
  123.4 20.4 %collective-permute-start.7 = (bf16[12,32,1024]{2,1,0:T(8,128)(2,1)}, bf16[12,32,1024]{2,1,0:T(8,128)(2,1)}, u32[]{:S(2)}, u32[]{:S(2)}) collective-permute-start(bf16[12,32,1024]{2,1,0:T(8,128)(2,1)} %get-tuple-element.21.own_ref), channel_id=1, source_target_pairs={{0,1},{3,2},{4,5},{7,6},{8,9},{11,10},{12,13},{15,14},{16,17},{19,... | collective-permute-start | bytes 2359304 | tf_op jit(solution)/shard_map/ppermute | solution.py:95
  153.7 29.5 %collective-permute-start.8 = (f32[8,32,1024]{2,1,0:T(8,128)}, f32[8,32,1024]{2,1,0:T(8,128)}, u32[]{:S(2)}, u32[]{:S(2)}) collective-permute-start(f32[8,32,1024]{2,1,0:T(8,128)} %shard_map.50), channel_id=1, source_target_pairs={{1,2},{2,1},{5,6},{6,5},{9,10},{10,9},{13,14},{14,13},{17,18},{18,... | collective-permute-start | bytes 3145736 | tf_op jit(solution)/shard_map/ppermute | solution.py:238
  155.3 18.1 %collective-permute-start.10 = (bf16[12,32,1024]{2,1,0:T(8,128)(2,1)}, bf16[12,32,1024]{2,1,0:T(8,128)(2,1)}, u32[]{:S(2)}, u32[]{:S(2)}) collective-permute-start(bf16[12,32,1024]{2,1,0:T(8,128)(2,1)} %get-tuple-element.23.own_ref), channel_id=1, source_target_pairs={{0,1},{3,2},{4,5},{7,6},{8,9},{11,10},{12,13},{15,14},{16,17},{19,... | collective-permute-start | bytes 2359304 | tf_op jit(solution)/shard_map/ppermute | solution.py:95
  183.2 29.5 %collective-permute-start.11 = (f32[8,32,1024]{2,1,0:T(8,128)}, f32[8,32,1024]{2,1,0:T(8,128)}, u32[]{:S(2)}, u32[]{:S(2)}) collective-permute-start(f32[8,32,1024]{2,1,0:T(8,128)} %shard_map.52), channel_id=1, source_target_pairs={{1,2},{2,1},{5,6},{6,5},{9,10},{10,9},{13,14},{14,13},{17,18},{18,... | collective-permute-start | bytes 3145736 | tf_op jit(solution)/shard_map/ppermute | solution.py:238
  184.8 18.0 %collective-permute-start.13 = (bf16[12,32,1024]{2,1,0:T(8,128)(2,1)}, bf16[12,32,1024]{2,1,0:T(8,128)(2,1)}, u32[]{:S(2)}, u32[]{:S(2)}) collective-permute-start(bf16[12,32,1024]{2,1,0:T(8,128)(2,1)} %get-tuple-element.25.own_ref), channel_id=1, source_target_pairs={{0,1},{3,2},{4,5},{7,6},{8,9},{11,10},{12,13},{15,14},{16,17},{19,... | collective-permute-start | bytes 2359304 | tf_op jit(solution)/shard_map/ppermute | solution.py:95
  212.7 26.8 %collective-permute-start.14 = (f32[8,32,1024]{2,1,0:T(8,128)}, f32[8,32,1024]{2,1,0:T(8,128)}, u32[]{:S(2)}, u32[]{:S(2)}) collective-permute-start(f32[8,32,1024]{2,1,0:T(8,128)} %shard_map.54), channel_id=1, source_target_pairs={{1,2},{2,1},{5,6},{6,5},{9,10},{10,9},{13,14},{14,13},{17,18},{18,... | collective-permute-start | bytes 3145736 | tf_op jit(solution)/shard_map/ppermute | solution.py:238
  214.3 15.4 %collective-permute-start.16 = (bf16[12,32,1024]{2,1,0:T(8,128)(2,1)S(1)}, bf16[12,32,1024]{2,1,0:T(8,128)(2,1)}, u32[]{:S(2)}, u32[]{:S(2)}) collective-permute-start(bf16[12,32,1024]{2,1,0:T(8,128)(2,1)S(1)} %get-tuple-element.27.own_ref), channel_id=1, source_target_pairs={{0,1},{3,2},{4,5},{7,6},{8,9},{11,10},{12,13},{15,14},{16,17},{19,... | collective-permute-start | bytes 2359304 | tf_op jit(solution)/shard_map/ppermute | solution.py:95
  239.5 28.2 %collective-permute-start.17 = (f32[8,32,1024]{2,1,0:T(8,128)}, f32[8,32,1024]{2,1,0:T(8,128)}, u32[]{:S(2)}, u32[]{:S(2)}) collective-permute-start(f32[8,32,1024]{2,1,0:T(8,128)} %shard_map.56), channel_id=1, source_target_pairs={{1,2},{2,1},{5,6},{6,5},{9,10},{10,9},{13,14},{14,13},{17,18},{18,... | collective-permute-start | bytes 3145736 | tf_op jit(solution)/shard_map/ppermute | solution.py:238
  241.2 15.8 %collective-permute-start.19 = (bf16[12,32,1024]{2,1,0:T(8,128)(2,1)S(1)}, bf16[12,32,1024]{2,1,0:T(8,128)(2,1)S(1)}, u32[]{:S(2)}, u32[]{:S(2)}) collective-permute-start(bf16[12,32,1024]{2,1,0:T(8,128)(2,1)S(1)} %get-tuple-element.29.own_ref), channel_id=1, source_target_pairs={{0,1},{3,2},{4,5},{7,6},{8,9},{11,10},{12,13},{15,14},{16,17},{19,... | collective-permute-start | bytes 2359304 | tf_op jit(solution)/shard_map/ppermute | solution.py:95
  267.7 27.1 %collective-permute-start.20 = (f32[8,32,1024]{2,1,0:T(8,128)}, f32[8,32,1024]{2,1,0:T(8,128)}, u32[]{:S(2)}, u32[]{:S(2)}) collective-permute-start(f32[8,32,1024]{2,1,0:T(8,128)} %shard_map.58), channel_id=1, source_target_pairs={{1,2},{2,1},{5,6},{6,5},{9,10},{10,9},{13,14},{14,13},{17,18},{18,... | collective-permute-start | bytes 3145736 | tf_op jit(solution)/shard_map/ppermute | solution.py:238
  269.3 27.3 %copy-start.22 = (f32[12,8,1024]{2,1,0:T(8,128)S(1)}, f32[12,8,1024]{2,1,0:T(8,128)}, u32[]{:S(2)}) copy-start(f32[12,8,1024]{2,1,0:T(8,128)} %get-tuple-element.50) | copy-start | bytes 1179652
  269.3 14.7 %collective-permute-start.22 = (bf16[12,32,1024]{2,1,0:T(8,128)(2,1)S(1)}, bf16[12,32,1024]{2,1,0:T(8,128)(2,1)S(1)}, u32[]{:S(2)}, u32[]{:S(2)}) collective-permute-start(bf16[12,32,1024]{2,1,0:T(8,128)(2,1)S(1)} %get-tuple-element.31.own_ref), channel_id=1, source_target_pairs={{0,1},{3,2},{4,5},{7,6},{8,9},{11,10},{12,13},{15,14},{16,17},{19,... | collective-permute-start | bytes 2359304 | tf_op jit(solution)/shard_map/ppermute | solution.py:95
  294.8 92.5 %collective-permute-start.23 = (f32[8,32,1024]{2,1,0:T(8,128)}, f32[8,32,1024]{2,1,0:T(8,128)}, u32[]{:S(2)}, u32[]{:S(2)}) collective-permute-start(f32[8,32,1024]{2,1,0:T(8,128)} %shard_map.60), channel_id=1, source_target_pairs={{1,2},{2,1},{5,6},{6,5},{9,10},{10,9},{13,14},{14,13},{17,18},{18,... | collective-permute-start | bytes 3145736 | tf_op jit(solution)/shard_map/ppermute | solution.py:238
  312.2 9.4 %copy-start.14 = (f32[8,32,1024]{2,1,0:T(8,128)}, f32[8,32,1024]{2,1,0:T(8,128)S(1)}, u32[]{:S(2)}) copy-start(f32[8,32,1024]{2,1,0:T(8,128)S(1)} %add.106) | copy-start | bytes 3145732
  313.1 46.5 %collective-permute-start.6 = (f32[4,32,1024]{2,1,0:T(8,128)}, f32[4,32,1024]{2,1,0:T(8,128)S(1)}, u32[]{:S(2)}, u32[]{:S(2)}) collective-permute-start(f32[4,32,1024]{2,1,0:T(8,128)} %slice.163), channel_id=1, source_target_pairs={{1,0},{2,3},{5,4},{6,7},{9,8},{10,11},{13,12},{14,15},{17,16},{18,... | collective-permute-start | bytes 1572872 | tf_op jit(solution)/shard_map/ppermute | solution.py:241
  314.4 63.1 %collective-permute-start.25 = (bf16[12,32,1024]{2,1,0:T(8,128)(2,1)S(1)}, bf16[12,32,1024]{2,1,0:T(8,128)(2,1)}, u32[]{:S(2)}, u32[]{:S(2)}) collective-permute-start(bf16[12,32,1024]{2,1,0:T(8,128)(2,1)S(1)} %get-tuple-element.33.own_ref), channel_id=1, source_target_pairs={{0,1},{3,2},{4,5},{7,6},{8,9},{11,10},{12,13},{15,14},{16,17},{19,... | collective-permute-start | bytes 2359304 | tf_op jit(solution)/shard_map/ppermute | solution.py:95
  333.1 1.2 copy-start.13
  334.3 54.7 %collective-permute-start.9 = (f32[4,32,1024]{2,1,0:T(8,128)}, f32[4,32,1024]{2,1,0:T(8,128)}, u32[]{:S(2)}, u32[]{:S(2)}) collective-permute-start(f32[4,32,1024]{2,1,0:T(8,128)} %slice.166), channel_id=1, source_target_pairs={{1,0},{2,3},{5,4},{6,7},{9,8},{10,11},{13,12},{14,15},{17,16},{18,... | collective-permute-start | bytes 1572872 | tf_op jit(solution)/shard_map/ppermute | solution.py:241
  354.6 5.0 %copy-start = (f32[512,1024]{1,0:T(8,128)S(1)}, f32[512,1024]{1,0:T(8,128)}, u32[]{:S(2)}) copy-start(f32[512,1024]{1,0:T(8,128)} %get-tuple-element.64) | copy-start | bytes 6291460
  354.6 5.0 %copy-start.15 = (f32[8,32,1024]{2,1,0:T(8,128)S(1)}, f32[8,32,1024]{2,1,0:T(8,128)}, u32[]{:S(2)}) copy-start(f32[8,32,1024]{2,1,0:T(8,128)} %copy-done.14) | copy-start | bytes 3145732
  358.3 50.8 %collective-permute-start.12 = (f32[4,32,1024]{2,1,0:T(8,128)}, f32[4,32,1024]{2,1,0:T(8,128)}, u32[]{:S(2)}, u32[]{:S(2)}) collective-permute-start(f32[4,32,1024]{2,1,0:T(8,128)} %slice.169), channel_id=1, source_target_pairs={{1,0},{2,3},{5,4},{6,7},{9,8},{10,11},{13,12},{14,15},{17,16},{18,... | collective-permute-start | bytes 1572872 | tf_op jit(solution)/shard_map/ppermute | solution.py:241
  376.2 61.9 %collective-permute-start.15 = (f32[4,32,1024]{2,1,0:T(8,128)}, f32[4,32,1024]{2,1,0:T(8,128)S(1)}, u32[]{:S(2)}, u32[]{:S(2)}) collective-permute-start(f32[4,32,1024]{2,1,0:T(8,128)} %slice.172), channel_id=1, source_target_pairs={{1,0},{2,3},{5,4},{6,7},{9,8},{10,11},{13,12},{14,15},{17,16},{18,... | collective-permute-start | bytes 1572872 | tf_op jit(solution)/shard_map/ppermute | solution.py:241
  387.3 70.4 %collective-permute-start.26 = (f32[8,32,1024]{2,1,0:T(8,128)}, f32[8,32,1024]{2,1,0:T(8,128)}, u32[]{:S(2)}, u32[]{:S(2)}) collective-permute-start(f32[8,32,1024]{2,1,0:T(8,128)} %shard_map.62), channel_id=1, source_target_pairs={{1,2},{2,1},{5,6},{6,5},{9,10},{10,9},{13,14},{14,13},{17,18},{18,... | collective-permute-start | bytes 3145736 | tf_op jit(solution)/shard_map/ppermute | solution.py:238
  403.9 5.2 %copy-start.1 = (f32[512,1024]{1,0:T(8,128)S(1)}, f32[512,1024]{1,0:T(8,128)}, u32[]{:S(2)}) copy-start(f32[512,1024]{1,0:T(8,128)} %get-tuple-element.64) | copy-start | bytes 6291460
  403.9 5.2 %copy-start.12 = (f32[8,32,1024]{2,1,0:T(8,128)S(1)}, f32[8,32,1024]{2,1,0:T(8,128)}, u32[]{:S(2)}) copy-start(f32[8,32,1024]{2,1,0:T(8,128)} %copy-done.11) | copy-start | bytes 3145732
  405.8 1.0 copy-start.16
  407.6 46.8 %collective-permute-start.18 = (f32[4,32,1024]{2,1,0:T(8,128)}, f32[4,32,1024]{2,1,0:T(8,128)S(1)}, u32[]{:S(2)}, u32[]{:S(2)}) collective-permute-start(f32[4,32,1024]{2,1,0:T(8,128)} %slice.175), channel_id=1, source_target_pairs={{1,0},{2,3},{5,4},{6,7},{9,8},{10,11},{13,12},{14,15},{17,16},{18,... | collective-permute-start | bytes 1572872 | tf_op jit(solution)/shard_map/ppermute | solution.py:241
  433.1 5.0 %copy-start.2 = (f32[512,1024]{1,0:T(8,128)S(1)}, f32[512,1024]{1,0:T(8,128)}, u32[]{:S(2)}) copy-start(f32[512,1024]{1,0:T(8,128)} %get-tuple-element.64) | copy-start | bytes 6291460
  433.1 5.0 %copy-start.10 = (f32[8,32,1024]{2,1,0:T(8,128)S(1)}, f32[8,32,1024]{2,1,0:T(8,128)}, u32[]{:S(2)}) copy-start(f32[8,32,1024]{2,1,0:T(8,128)} %copy-done.9) | copy-start | bytes 3145732
  436.8 24.0 %collective-permute-start.21 = (f32[4,32,1024]{2,1,0:T(8,128)}, f32[4,32,1024]{2,1,0:T(8,128)}, u32[]{:S(2)}, u32[]{:S(2)}) collective-permute-start(f32[4,32,1024]{2,1,0:T(8,128)} %slice.178), channel_id=1, source_target_pairs={{1,0},{2,3},{5,4},{6,7},{9,8},{10,11},{13,12},{14,15},{17,16},{18,... | collective-permute-start | bytes 1572872 | tf_op jit(solution)/shard_map/ppermute | solution.py:241
  451.1 3.3 copy-start.3
  451.1 3.4 copy-start.17
  453.0 4.7 copy-start.8
  453.0 13.4 %collective-permute-start.24 = (f32[4,32,1024]{2,1,0:T(8,128)S(1)}, f32[4,32,1024]{2,1,0:T(8,128)S(1)}, u32[]{:S(2)}, u32[]{:S(2)}) collective-permute-start(f32[4,32,1024]{2,1,0:T(8,128)S(1)} %slice.181), channel_id=1, source_target_pairs={{1,0},{2,3},{5,4},{6,7},{9,8},{10,11},{13,12},{14,15},{17,16},{18,... | collective-permute-start | bytes 1572872 | tf_op jit(solution)/shard_map/ppermute | solution.py:241
  457.7 3.1 copy-start.19
  459.2 13.1 %collective-permute-start.27 = (f32[4,32,1024]{2,1,0:T(8,128)S(1)}, f32[4,32,1024]{2,1,0:T(8,128)S(1)}, u32[]{:S(2)}, u32[]{:S(2)}) collective-permute-start(f32[4,32,1024]{2,1,0:T(8,128)S(1)} %slice.184), channel_id=1, source_target_pairs={{1,0},{2,3},{5,4},{6,7},{9,8},{10,11},{13,12},{14,15},{17,16},{18,... | collective-permute-start | bytes 1572872 | tf_op jit(solution)/shard_map/ppermute | solution.py:241
  (5 other events, 4.7 us)
where the time goes:
time: 485 us; the launch traced here: 476 us
  Pallas kernels  173 us (36%)
  waiting for transfers between devices  99.9 us (21%)
  starting transfers between devices  83.4 us (17%)
  other arithmetic  37.6 us (8%)
  local copies, waits for them, and re-layouts  36.3 us (7%)
  matrix products  29.6 us (6%)
  between operations  16.6 us (3%)
    pallas_call x16, Pallas kernels, cross_chunk(): pl.pallas_call(cross_kernel, grid=(width // step_rows,), in_specs=[pl.Blo...  157 us
    ppermute x9, waiting for transfers between devices, edge_first(): return lax.ppermute(values, 'tm', [(0, 1), (groups - 1, groups - 2)])  85 us
    ppermute x9, starting transfers between devices, edge_first(): return lax.ppermute(values, 'tm', [(0, 1), (groups - 1, groups - 2)])  53.9 us
    dot_general x8, matrix products, on_line(): outs.append(jnp.dot(final, inverse, precision=lax.Precision.HIGHEST))  29.6 us
    pallas_call x1, Pallas kernels, whiten_segments(): pl.pallas_call(whiten_kernel, grid=(segments,), in_specs=[pl.BlockSpec((N...  15.3 us
    add x8, other arithmetic, on_line(): total = cross_chunk(own, edge_rows, near_wide, edge_near_wide) + got  13.8 us
    unnamed x51, local copies, waits for them, and re-layouts  13.7 us
    ppermute x8, starting transfers between devices, on_line(): got = lax.ppermute(far_part, 'tm', [(1, 2), (2, 1)])  13.3 us
  transfers between devices with their start and end apart: 28, of which 12 were waited for; matrix products, arithmetic and copies ran while one was open for 14% of the time, Pallas kernels for 31%

commit v1 on v0

--- a/solution.py
+++ b/solution.py
@@ -125,30 +125,33 @@
 def cross_kernel(own_ref, edge_ref, own_src_ref, edge_src_ref, out_ref):
     segments = own_ref.shape[0]
     sources = own_src_ref.shape[1]
+    rows = own_ref.shape[1]
     bins = own_ref.shape[-1] // 2
-    for half in range(own_ref.shape[1] // ROWS):
-        rows = pl.ds(half * ROWS, ROWS)
-        for tile in range(bins // LANES):
-            re_lanes = pl.ds(tile * LANES, LANES)
-            im_lanes = pl.ds(bins + tile * LANES, LANES)
-
-            def step(m, acc, data_ref, src_ref):
-                wr = data_ref[m, rows, re_lanes].astype(jnp.float32)
-                wi = data_ref[m, rows, im_lanes].astype(jnp.float32)
-                out = []
-                for j in range(sources):
-                    sr = src_ref[m, j, :, re_lanes]
-                    si = src_ref[m, j, :, im_lanes]
-                    out.append(acc[2 * j] + (wr * sr + wi * si))
-                    out.append(acc[2 * j + 1] + (wi * sr - wr * si))
-                return tuple(out)
-
-            acc = tuple(jnp.zeros((ROWS, LANES), jnp.float32) for _ in range(2 * sources))
-            acc = lax.fori_loop(0, segments, lambda m, a: step(m, a, own_ref, own_src_ref), acc)
-            acc = lax.fori_loop(0, segments, lambda m, a: step(m, a, edge_ref, edge_src_ref), acc)
+
+    def tile_body(tile, carry):
+        re_lanes = pl.ds(pl.multiple_of(tile * LANES, LANES), LANES)
+        im_lanes = pl.ds(pl.multiple_of(bins + tile * LANES, LANES), LANES)
+
+        def step(m, acc, data_ref, src_ref):
+            wr = data_ref[m, :, re_lanes].astype(jnp.float32)
+            wi = data_ref[m, :, im_lanes].astype(jnp.float32)
+            out = []
             for j in range(sources):
-                out_ref[j, rows, re_lanes] = acc[2 * j]
-                out_ref[j, rows, im_lanes] = acc[2 * j + 1]
+                sr = jnp.concatenate([src_ref[m, j, :, re_lanes]] * (rows // ROWS), axis=0)
+                si = jnp.concatenate([src_ref[m, j, :, im_lanes]] * (rows // ROWS), axis=0)
+                out.append(acc[2 * j] + (wr * sr + wi * si))
+                out.append(acc[2 * j + 1] + (wi * sr - wr * si))
+            return tuple(out)
+
+        acc = tuple(jnp.zeros((rows, LANES), jnp.float32) for _ in range(2 * sources))
+        acc = lax.fori_loop(0, segments, lambda m, a: step(m, a, own_ref, own_src_ref), acc)
+        acc = lax.fori_loop(0, segments, lambda m, a: step(m, a, edge_ref, edge_src_ref), acc)
+        for j in range(sources):
+            out_ref[j, :, re_lanes] = acc[2 * j]
+            out_ref[j, :, im_lanes] = acc[2 * j + 1]
+        return carry
+
+    lax.fori_loop(0, bins // LANES, tile_body, 0)
 
 
 def cross_chunk(own, edge, own_src, edge_src):

time: 485 us -> 476 us (0.981); the launches traced: 476 us -> 474 us
  no operation moved by 1% of the time
where the time goes in v1:
time: 476 us; the launch traced here: 474 us
  Pallas kernels  172 us (36%)
  waiting for transfers between devices  99.5 us (21%)
  starting transfers between devices  83.4 us (18%)
  other arithmetic  37.7 us (8%)
  local copies, waits for them, and re-layouts  36.3 us (8%)
  matrix products  29.6 us (6%)
  between operations  16.2 us (3%)
    pallas_call x16, Pallas kernels, cross_chunk(): pl.pallas_call(cross_kernel, grid=(width // step_rows,), in_specs=[pl.Blo...  156 us
    ppermute x9, waiting for transfers between devices, edge_first(): return lax.ppermute(values, 'tm', [(0, 1), (groups - 1, groups - 2)])  85 us
    ppermute x9, starting transfers between devices, edge_first(): return lax.ppermute(values, 'tm', [(0, 1), (groups - 1, groups - 2)])  53.9 us
    dot_general x8, matrix products, on_line(): outs.append(jnp.dot(final, inverse, precision=lax.Precision.HIGHEST))  29.6 us
    pallas_call x1, Pallas kernels, whiten_segments(): pl.pallas_call(whiten_kernel, grid=(segments,), in_specs=[pl.BlockSpec((N...  15.3 us
    add x8, other arithmetic, on_line(): total = cross_chunk(own, edge_rows, near_wide, edge_near_wide) + got  13.8 us
    unnamed x51, local copies, waits for them, and re-layouts  13.7 us
    ppermute x8, starting transfers between devices, on_line(): got = lax.ppermute(far_part, 'tm', [(1, 2), (2, 1)])  13.2 us
  transfers between devices with their start and end apart: 28, of which 12 were waited for; matrix products, arithmetic and copies ran while one was open for 14% of the time, Pallas kernels for 31%

profile of v1, /device:TPU:0, one launch (start us, length us, event | category | flops | bytes accessed | tf_op | source)
XLA Modules:
  0.0 474.3 jit_solution(12221975331724120745)
XLA Ops:
  14.5 8.5 %negate_convert_fusion = (bf16[1024,512]{1,0:T(8,128)(2,1)S(1)}, bf16[1024,512]{1,0:T(8,128)(2,1)S(1)}) fusion(), kind=kLoop, calls=%fused_computation.18 | loop fusion | flops 8912896 | bytes 2097152 | tf_op jit(solution)/shard_map/convert.1
  26.4 7.6 %copy.7 = bf16[256,2,6,1024]{3,0,2,1:T(8,128)(2,1)} copy(bf16[256,2,6,1024]{3,1,2,0:T(2,128)(2,1)} %param.4) | data formatting | bytes 12582912 | tf_op args[0]
  37.3 15.3 %shard_map.46 = bf16[8,12,32,1024]{3,2,1,0:T(8,128)(2,1)} custom-call(bf16[12,256,1024]{2,1,0:T(8,128)(2,1)} %bitcast.50, bf16[1024,1024]{1,0:T(8,128)(2,1)} %pad_maximum_fusion.forward_ref, f32[12,256,1]{2,1,0:T(8,128)} %copy.9.mask_ref), custom_call_target="tpu_custom_call" | custom-call | tf_op jit(solution)/shard_map/pallas_call | solution.py:108
  56.6 2.9 collective-permute-start.2
  59.6 9.4 %collective-permute-done.2 = bf16[12,16,1024]{2,1,0:T(8,128)(2,1)S(1)} collective-permute-done((bf16[12,16,1024]{2,1,0:T(8,128)(2,1)S(1)}, bf16[12,16,1024]{2,1,0:T(8,128)(2,1)S(1)}, u32[]{:S(2)}, u32[]{:S(2)}) %collective-permute-start.2) | collective-permute-done | bytes 393248 | tf_op jit(solution)/shard_map/ppermute | solution.py:179
  71.0 5.1 %slice_bitcast_fusion = (bf16[12,32,1024]{2,1,0:T(8,128)(2,1)S(1)}, bf16[12,32,1024]{2,1,0:T(8,128)(2,1)S(1)}, bf16[12,32,1024]{2,1,0:T(8,128)(2,1)S(1)}, bf16[1...) fusion(bf16[8,12,32,1024]{3,2,1,0:T(8,128)(2,1)} %shard_map.46), kind=kLoop, calls=%fused_computation.32 | loop fusion | bytes 12582912 | tf_op jit(solution)/shard_map/squeeze | solution.py:236
  76.1 4.4 collective-permute-start
  81.9 14.0 %collective-permute-done.edge_ref = bf16[12,32,1024]{2,1,0:T(8,128)(2,1)} collective-permute-done((bf16[12,32,1024]{2,1,0:T(8,128)(2,1)}, bf16[12,32,1024]{2,1,0:T(8,128)(2,1)}, u32[]{:S(2)}, u32[]{:S(2)}) %collective-permute-start) | collective-permute-done | bytes 786464 | tf_op jit(solution)/shard_map/ppermute | solution.py:95
  95.9 4.4 collective-permute-start.4
  100.3 6.6 %collective-permute-done.4 = bf16[12,16,1024]{2,1,0:T(8,128)(2,1)S(1)} collective-permute-done((bf16[12,16,1024]{2,1,0:T(8,128)(2,1)S(1)}, bf16[12,16,1024]{2,1,0:T(8,128)(2,1)S(1)}, u32[]{:S(2)}, u32[]{:S(2)}) %collective-permute-start.4) | collective-permute-done | bytes 393248 | tf_op jit(solution)/shard_map/ppermute | solution.py:95
  112.0 9.8 %shard_map.48 = f32[8,32,1024]{2,1,0:T(8,128)} custom-call(bf16[12,32,1024]{2,1,0:T(8,128)(2,1)} %get-tuple-element.42.own_ref, bf16[12,32,1024]{2,1,0:T(8,128)(2,1)} %collective-permute-done.edge_ref, f32[12,8,8,1024]{3,2,1,0:T(8,128)} %broadcast_in_dim.51.own_src_ref, f32[12,8,8,1024]{3,2,1,0:T(8,128)} %broadcast_in_dim.52.edge_src_ref), custom_call_target="tpu_custom_call" | custom-call | tf_op jit(solution)/shard_map/pallas_call | solution.py:161
  123.4 7.1 %collective-permute-start.7 = (bf16[12,32,1024]{2,1,0:T(8,128)(2,1)}, bf16[12,32,1024]{2,1,0:T(8,128)(2,1)}, u32[]{:S(2)}, u32[]{:S(2)}) collective-permute-start(bf16[12,32,1024]{2,1,0:T(8,128)(2,1)} %get-tuple-element.21.own_ref), channel_id=1, source_target_pairs={{0,1},{3,2},{4,5},{7,6},{8,9},{11,10},{12,13},{15,14},{16,17},{19,... | collective-permute-start | bytes 2359304 | tf_op jit(solution)/shard_map/ppermute | solution.py:95
  130.5 13.3 %collective-permute-done.7.edge_ref = bf16[12,32,1024]{2,1,0:T(8,128)(2,1)} collective-permute-done((bf16[12,32,1024]{2,1,0:T(8,128)(2,1)}, bf16[12,32,1024]{2,1,0:T(8,128)(2,1)}, u32[]{:S(2)}, u32[]{:S(2)}) %collective-permute-start.7) | collective-permute-done | bytes 786464 | tf_op jit(solution)/shard_map/ppermute | solution.py:95
  143.8 9.8 %shard_map.50 = f32[8,32,1024]{2,1,0:T(8,128)} custom-call(bf16[12,32,1024]{2,1,0:T(8,128)(2,1)} %get-tuple-element.21.own_ref, bf16[12,32,1024]{2,1,0:T(8,128)(2,1)} %collective-permute-done.7.edge_ref, f32[12,8,8,1024]{3,2,1,0:T(8,128)} %broadcast_in_dim.51.own_src_ref, f32[12,8,8,1024]{3,2,1,0:T(8,128)} %broadcast_in_dim.52.edge_src_ref), custom_call_target="tpu_custom_call" | custom-call | tf_op jit(solution)/shard_map/pallas_call | solution.py:161
  155.2 6.0 %collective-permute-start.10 = (bf16[12,32,1024]{2,1,0:T(8,128)(2,1)}, bf16[12,32,1024]{2,1,0:T(8,128)(2,1)}, u32[]{:S(2)}, u32[]{:S(2)}) collective-permute-start(bf16[12,32,1024]{2,1,0:T(8,128)(2,1)} %get-tuple-element.23.own_ref), channel_id=1, source_target_pairs={{0,1},{3,2},{4,5},{7,6},{8,9},{11,10},{12,13},{15,14},{16,17},{19,... | collective-permute-start | bytes 2359304 | tf_op jit(solution)/shard_map/ppermute | solution.py:95
  161.2 12.0 %collective-permute-done.10.edge_ref = bf16[12,32,1024]{2,1,0:T(8,128)(2,1)} collective-permute-done((bf16[12,32,1024]{2,1,0:T(8,128)(2,1)}, bf16[12,32,1024]{2,1,0:T(8,128)(2,1)}, u32[]{:S(2)}, u32[]{:S(2)}) %collective-permute-start.10) | collective-permute-done | bytes 786464 | tf_op jit(solution)/shard_map/ppermute | solution.py:95
  173.3 9.8 %shard_map.52 = f32[8,32,1024]{2,1,0:T(8,128)} custom-call(bf16[12,32,1024]{2,1,0:T(8,128)(2,1)} %get-tuple-element.23.own_ref, bf16[12,32,1024]{2,1,0:T(8,128)(2,1)} %collective-permute-done.10.edge_ref, f32[12,8,8,1024]{3,2,1,0:T(8,128)} %broadcast_in_dim.51.own_src_ref, f32[12,8,8,1024]{3,2,1,0:T(8,128)} %broadcast_in_dim.52.edge_src_ref), custom_call_target="tpu_custom_call" | custom-call | tf_op jit(solution)/shard_map/pallas_call | solution.py:161
  184.7 7.1 %collective-permute-start.13 = (bf16[12,32,1024]{2,1,0:T(8,128)(2,1)}, bf16[12,32,1024]{2,1,0:T(8,128)(2,1)}, u32[]{:S(2)}, u32[]{:S(2)}) collective-permute-start(bf16[12,32,1024]{2,1,0:T(8,128)(2,1)} %get-tuple-element.25.own_ref), channel_id=1, source_target_pairs={{0,1},{3,2},{4,5},{7,6},{8,9},{11,10},{12,13},{15,14},{16,17},{19,... | collective-permute-start | bytes 2359304 | tf_op jit(solution)/shard_map/ppermute | solution.py:95
  191.8 10.9 %collective-permute-done.13.edge_ref = bf16[12,32,1024]{2,1,0:T(8,128)(2,1)} collective-permute-done((bf16[12,32,1024]{2,1,0:T(8,128)(2,1)}, bf16[12,32,1024]{2,1,0:T(8,128)(2,1)}, u32[]{:S(2)}, u32[]{:S(2)}) %collective-permute-start.13) | collective-permute-done | bytes 786464 | tf_op jit(solution)/shard_map/ppermute | solution.py:95
  202.7 9.8 %shard_map.54 = f32[8,32,1024]{2,1,0:T(8,128)} custom-call(bf16[12,32,1024]{2,1,0:T(8,128)(2,1)} %get-tuple-element.25.own_ref, bf16[12,32,1024]{2,1,0:T(8,128)(2,1)} %collective-permute-done.13.edge_ref, f32[12,8,8,1024]{3,2,1,0:T(8,128)} %broadcast_in_dim.51.own_src_ref, f32[12,8,8,1024]{3,2,1,0:T(8,128)} %broadcast_in_dim.52.edge_src_ref), custom_call_target="tpu_custom_call" | custom-call | tf_op jit(solution)/shard_map/pallas_call | solution.py:161
  214.1 6.0 %collective-permute-start.16 = (bf16[12,32,1024]{2,1,0:T(8,128)(2,1)S(1)}, bf16[12,32,1024]{2,1,0:T(8,128)(2,1)}, u32[]{:S(2)}, u32[]{:S(2)}) collective-permute-start(bf16[12,32,1024]{2,1,0:T(8,128)(2,1)S(1)} %get-tuple-element.27.own_ref), channel_id=1, source_target_pairs={{0,1},{3,2},{4,5},{7,6},{8,9},{11,10},{12,13},{15,14},{16,17},{19,... | collective-permute-start | bytes 2359304 | tf_op jit(solution)/shard_map/ppermute | solution.py:95
  220.1 9.4 %collective-permute-done.16.edge_ref = bf16[12,32,1024]{2,1,0:T(8,128)(2,1)} collective-permute-done((bf16[12,32,1024]{2,1,0:T(8,128)(2,1)S(1)}, bf16[12,32,1024]{2,1,0:T(8,128)(2,1)}, u32[]{:S(2)}, u32[]{:S(2)}) %collective-permute-start.16) | collective-permute-done | bytes 786464 | tf_op jit(solution)/shard_map/ppermute | solution.py:95
  229.5 9.8 %shard_map.56 = f32[8,32,1024]{2,1,0:T(8,128)} custom-call(bf16[12,32,1024]{2,1,0:T(8,128)(2,1)} %copy-done.7, bf16[12,32,1024]{2,1,0:T(8,128)(2,1)} %collective-permute-done.16.edge_ref, f32[12,8,8,1024]{3,2,1,0:T(8,128)} %broadcast_in_dim.51.own_src_ref, f32[12,8,8,1024]{3,2,1,0:T(8,128)} %broadcast_in_dim.52.edge_src_ref), custom_call_target="tpu_custom_call" | custom-call | tf_op jit(solution)/shard_map/pallas_call | solution.py:161
  241.0 6.3 %collective-permute-start.19 = (bf16[12,32,1024]{2,1,0:T(8,128)(2,1)S(1)}, bf16[12,32,1024]{2,1,0:T(8,128)(2,1)S(1)}, u32[]{:S(2)}, u32[]{:S(2)}) collective-permute-start(bf16[12,32,1024]{2,1,0:T(8,128)(2,1)S(1)} %get-tuple-element.29.own_ref), channel_id=1, source_target_pairs={{0,1},{3,2},{4,5},{7,6},{8,9},{11,10},{12,13},{15,14},{16,17},{19,... | collective-permute-start | bytes 2359304 | tf_op jit(solution)/shard_map/ppermute | solution.py:95
  247.3 9.4 %collective-permute-done.19.edge_ref = bf16[12,32,1024]{2,1,0:T(8,128)(2,1)S(1)} collective-permute-done((bf16[12,32,1024]{2,1,0:T(8,128)(2,1)S(1)}, bf16[12,32,1024]{2,1,0:T(8,128)(2,1)S(1)}, u32[]{:S(2)}, u32[]{:S(2)}) %collective-permute-start.19) | collective-permute-done | bytes 786464 | tf_op jit(solution)/shard_map/ppermute | solution.py:95
  257.6 9.8 %shard_map.58 = f32[8,32,1024]{2,1,0:T(8,128)} custom-call(bf16[12,32,1024]{2,1,0:T(8,128)(2,1)} %copy-done.6, bf16[12,32,1024]{2,1,0:T(8,128)(2,1)} %copy-done.20, f32[12,8,8,1024]{3,2,1,0:T(8,128)} %broadcast_in_dim.51.own_src_ref, f32[12,8,8,1024]{3,2,1,0:T(8,128)} %broadcast_in_dim.52.edge_src_ref), custom_call_target="tpu_custom_call" | custom-call | tf_op jit(solution)/shard_map/pallas_call | solution.py:161
  269.0 5.3 %collective-permute-start.22 = (bf16[12,32,1024]{2,1,0:T(8,128)(2,1)S(1)}, bf16[12,32,1024]{2,1,0:T(8,128)(2,1)S(1)}, u32[]{:S(2)}, u32[]{:S(2)}) collective-permute-start(bf16[12,32,1024]{2,1,0:T(8,128)(2,1)S(1)} %get-tuple-element.31.own_ref), channel_id=1, source_target_pairs={{0,1},{3,2},{4,5},{7,6},{8,9},{11,10},{12,13},{15,14},{16,17},{19,... | collective-permute-start | bytes 2359304 | tf_op jit(solution)/shard_map/ppermute | solution.py:95
  274.3 9.4 %collective-permute-done.22.edge_ref = bf16[12,32,1024]{2,1,0:T(8,128)(2,1)S(1)} collective-permute-done((bf16[12,32,1024]{2,1,0:T(8,128)(2,1)S(1)}, bf16[12,32,1024]{2,1,0:T(8,128)(2,1)S(1)}, u32[]{:S(2)}, u32[]{:S(2)}) %collective-permute-start.22) | collective-permute-done | bytes 786464 | tf_op jit(solution)/shard_map/ppermute | solution.py:95
  284.7 9.8 %shard_map.60 = f32[8,32,1024]{2,1,0:T(8,128)} custom-call(bf16[12,32,1024]{2,1,0:T(8,128)(2,1)} %copy-done.5, bf16[12,32,1024]{2,1,0:T(8,128)(2,1)} %copy-done.21, f32[12,8,8,1024]{3,2,1,0:T(8,128)} %broadcast_in_dim.51.own_src_ref, f32[12,8,8,1024]{3,2,1,0:T(8,128)} %broadcast_in_dim.52.edge_src_ref), custom_call_target="tpu_custom_call" | custom-call | tf_op jit(solution)/shard_map/pallas_call | solution.py:161
  300.2 9.8 %shard_map.47 = f32[8,32,1024]{2,1,0:T(8,128)} custom-call(bf16[12,32,1024]{2,1,0:T(8,128)(2,1)} %get-tuple-element.42.own_ref, bf16[12,32,1024]{2,1,0:T(8,128)(2,1)} %collective-permute-done.edge_ref, f32[12,8,8,1024]{3,2,1,0:T(8,128)} %broadcast_in_dim.27.own_src_ref, f32[12,8,8,1024]{3,2,1,0:T(8,128)} %broadcast_in_dim.50.edge_src_ref), custom_call_target="tpu_custom_call" | custom-call | tf_op jit(solution)/shard_map/pallas_call | solution.py:161
  313.9 7.1 %collective-permute-start.25 = (bf16[12,32,1024]{2,1,0:T(8,128)(2,1)S(1)}, bf16[12,32,1024]{2,1,0:T(8,128)(2,1)}, u32[]{:S(2)}, u32[]{:S(2)}) collective-permute-start(bf16[12,32,1024]{2,1,0:T(8,128)(2,1)S(1)} %get-tuple-element.33.own_ref), channel_id=1, source_target_pairs={{0,1},{3,2},{4,5},{7,6},{8,9},{11,10},{12,13},{15,14},{16,17},{19,... | collective-permute-start | bytes 2359304 | tf_op jit(solution)/shard_map/ppermute | solution.py:95
  321.0 9.8 %shard_map.49 = f32[8,32,1024]{2,1,0:T(8,128)} custom-call(bf16[12,32,1024]{2,1,0:T(8,128)(2,1)} %get-tuple-element.21.own_ref, bf16[12,32,1024]{2,1,0:T(8,128)(2,1)} %collective-permute-done.7.edge_ref, f32[12,8,8,1024]{3,2,1,0:T(8,128)} %broadcast_in_dim.27.own_src_ref, f32[12,8,8,1024]{3,2,1,0:T(8,128)} %broadcast_in_dim.50.edge_src_ref), custom_call_target="tpu_custom_call" | custom-call | tf_op jit(solution)/shard_map/pallas_call | solution.py:161
  335.1 9.2 %sine_multiply_fusion = (f32[512,1024]{1,0:T(8,128)S(1)}, f32[512,1024]{1,0:T(8,128)}) fusion(f32[512]{0:T(512)S(1)} %fusion.20, f32[512]{0:T(512)S(1)} %select_multiply_fusion), kind=kLoop, calls=%fused_computation.14 | loop fusion | flops 8388608 | bytes 4198400 | tf_op jit(solution)/shard_map/mul | solution.py:35
  344.3 9.8 %shard_map.51 = f32[8,32,1024]{2,1,0:T(8,128)} custom-call(bf16[12,32,1024]{2,1,0:T(8,128)(2,1)} %get-tuple-element.23.own_ref, bf16[12,32,1024]{2,1,0:T(8,128)(2,1)} %collective-permute-done.10.edge_ref, f32[12,8,8,1024]{3,2,1,0:T(8,128)} %broadcast_in_dim.27.own_src_ref, f32[12,8,8,1024]{3,2,1,0:T(8,128)} %broadcast_in_dim.50.edge_src_ref), custom_call_target="tpu_custom_call" | custom-call | tf_op jit(solution)/shard_map/pallas_call | solution.py:161
  359.2 3.2 convolution_dynamic-update-slice_fusion.7
  362.4 9.8 %shard_map.53 = f32[8,32,1024]{2,1,0:T(8,128)} custom-call(bf16[12,32,1024]{2,1,0:T(8,128)(2,1)} %get-tuple-element.25.own_ref, bf16[12,32,1024]{2,1,0:T(8,128)(2,1)} %collective-permute-done.13.edge_ref, f32[12,8,8,1024]{3,2,1,0:T(8,128)} %broadcast_in_dim.27.own_src_ref, f32[12,8,8,1024]{3,2,1,0:T(8,128)} %broadcast_in_dim.50.edge_src_ref), custom_call_target="tpu_custom_call" | custom-call | tf_op jit(solution)/shard_map/pallas_call | solution.py:161
  377.0 9.8 %shard_map.62 = f32[8,32,1024]{2,1,0:T(8,128)} custom-call(bf16[12,32,1024]{2,1,0:T(8,128)(2,1)} %copy-done.4, bf16[12,32,1024]{2,1,0:T(8,128)(2,1)} %collective-permute-done.25.edge_ref, f32[12,8,8,1024]{3,2,1,0:T(8,128)} %broadcast_in_dim.51.own_src_ref, f32[12,8,8,1024]{3,2,1,0:T(8,128)} %broadcast_in_dim.52.edge_src_ref), custom_call_target="tpu_custom_call" | custom-call | tf_op jit(solution)/shard_map/pallas_call | solution.py:161
  388.4 5.1 %convolution_dynamic-update-slice_fusion.6 = f32[4,256,1024]{2,1,0:T(8,128)} fusion(f32[4,256,1024]{2,1,0:T(8,128)} %convolution_dynamic-update-slice_fusion.7, f32[4,32,1024]{2,1,0:T(8,128)} %collective-permute-done.9, f32[8,32,1024]{2,1,0:T(8,128)} %copy-done.13, pred[]{:T(512)S(6)} %or.3, f32[512,1024]{1,0:T(8,128)S(1)} %get-tuple-element.63, ...), kind=kOutput, calls=%fused_computation.30 | convolution fusion | flops 1611792384 | bytes 5767169 | tf_op jit(solution)/shard_map/dot_general | solution.py:246
  393.5 9.8 %shard_map.55 = f32[8,32,1024]{2,1,0:T(8,128)} custom-call(bf16[12,32,1024]{2,1,0:T(8,128)(2,1)} %copy-done.7, bf16[12,32,1024]{2,1,0:T(8,128)(2,1)} %collective-permute-done.16.edge_ref, f32[12,8,8,1024]{3,2,1,0:T(8,128)} %broadcast_in_dim.27.own_src_ref, f32[12,8,8,1024]{3,2,1,0:T(8,128)} %broadcast_in_dim.50.edge_src_ref), custom_call_target="tpu_custom_call" | custom-call | tf_op jit(solution)/shard_map/pallas_call | solution.py:161
  408.3 4.3 convolution_dynamic-update-slice_fusion.5
  412.6 9.8 %shard_map.57 = f32[8,32,1024]{2,1,0:T(8,128)} custom-call(bf16[12,32,1024]{2,1,0:T(8,128)(2,1)} %copy-done.6, bf16[12,32,1024]{2,1,0:T(8,128)(2,1)} %copy-done.20, f32[12,8,8,1024]{3,2,1,0:T(8,128)} %broadcast_in_dim.27.own_src_ref, f32[12,8,8,1024]{3,2,1,0:T(8,128)} %broadcast_in_dim.50.edge_src_ref), custom_call_target="tpu_custom_call" | custom-call | tf_op jit(solution)/shard_map/pallas_call | solution.py:161
  422.3 9.8 %shard_map.59 = f32[8,32,1024]{2,1,0:T(8,128)} custom-call(bf16[12,32,1024]{2,1,0:T(8,128)(2,1)} %copy-done.5, bf16[12,32,1024]{2,1,0:T(8,128)(2,1)} %copy-done.21, f32[12,8,8,1024]{3,2,1,0:T(8,128)} %broadcast_in_dim.27.own_src_ref, f32[12,8,8,1024]{3,2,1,0:T(8,128)} %broadcast_in_dim.50.edge_src_ref), custom_call_target="tpu_custom_call" | custom-call | tf_op jit(solution)/shard_map/pallas_call | solution.py:161
  437.4 3.2 convolution_dynamic-update-slice_fusion.4
  440.6 9.8 %shard_map.61 = f32[8,32,1024]{2,1,0:T(8,128)} custom-call(bf16[12,32,1024]{2,1,0:T(8,128)(2,1)} %copy-done.4, bf16[12,32,1024]{2,1,0:T(8,128)(2,1)} %collective-permute-done.25.edge_ref, f32[12,8,8,1024]{3,2,1,0:T(8,128)} %broadcast_in_dim.27.own_src_ref, f32[12,8,8,1024]{3,2,1,0:T(8,128)} %broadcast_in_dim.50.edge_src_ref), custom_call_target="tpu_custom_call" | custom-call | tf_op jit(solution)/shard_map/pallas_call | solution.py:161
  453.7 3.2 convolution_dynamic-update-slice_fusion.3
  460.0 4.2 convolution_dynamic-update-slice_fusion.2
  465.2 3.2 convolution_dynamic-update-slice_fusion.1
  471.1 3.2 convolution_dynamic-update-slice_fusion
  (125 shorter events, 75.1 us)
Async XLA Ops:
  0.0 23.1 %copy-start.24 = (s32[4]{0:T(128)S(1)}, s32[4]{0:T(128)}, u32[]{:S(2)}) copy-start(s32[4]{0:T(128)} %param.6) | copy-start | bytes 52
  26.4 7.6 %copy-start.23 = (s32[256,2,6]{0,1,2:T(2,128)S(1)}, s32[256,2,6]{0,1,2:T(2,128)}, u32[]{:S(2)}) copy-start(s32[256,2,6]{0,1,2:T(2,128)} %param.5) | copy-start | bytes 36868
  54.5 1.9 collective-permute-start.1
  56.6 12.3 %collective-permute-start.2 = (bf16[12,16,1024]{2,1,0:T(8,128)(2,1)S(1)}, bf16[12,16,1024]{2,1,0:T(8,128)(2,1)S(1)}, u32[]{:S(2)}, u32[]{:S(2)}) collective-permute-start(bf16[12,16,1024]{2,1,0:T(8,128)(2,1)S(1)} %fusion.21), channel_id=1, source_target_pairs={{0,8},{4,12},{8,0},{12,4},{16,24},{20,28},{24,16},{28,20},{1,9},{5... | collective-permute-start | bytes 1179656 | tf_op jit(solution)/shard_map/ppermute | solution.py:179
  69.1 11.4 %collective-permute-start.3 = (bf16[12,16,1024]{2,1,0:T(8,128)(2,1)S(1)}, bf16[12,16,1024]{2,1,0:T(8,128)(2,1)}, u32[]{:S(2)}, u32[]{:S(2)}) collective-permute-start(bf16[12,16,1024]{2,1,0:T(8,128)(2,1)S(1)} %add.104), channel_id=1, source_target_pairs={{0,16},{4,20},{8,24},{12,28},{16,0},{20,4},{24,8},{28,12},{1,17},{... | collective-permute-start | bytes 1179656 | tf_op jit(solution)/shard_map/ppermute | solution.py:179
  76.1 138.0 %copy-start.7 = (bf16[12,32,1024]{2,1,0:T(8,128)(2,1)}, bf16[12,32,1024]{2,1,0:T(8,128)(2,1)S(1)}, u32[]{:S(2)}) copy-start(bf16[12,32,1024]{2,1,0:T(8,128)(2,1)S(1)} %get-tuple-element.27.own_ref) | copy-start | bytes 2359300
  76.1 164.8 %copy-start.6 = (bf16[12,32,1024]{2,1,0:T(8,128)(2,1)}, bf16[12,32,1024]{2,1,0:T(8,128)(2,1)S(1)}, u32[]{:S(2)}) copy-start(bf16[12,32,1024]{2,1,0:T(8,128)(2,1)S(1)} %get-tuple-element.29.own_ref) | copy-start | bytes 2359300
  76.1 192.9 %copy-start.5 = (bf16[12,32,1024]{2,1,0:T(8,128)(2,1)}, bf16[12,32,1024]{2,1,0:T(8,128)(2,1)S(1)}, u32[]{:S(2)}) copy-start(bf16[12,32,1024]{2,1,0:T(8,128)(2,1)S(1)} %get-tuple-element.31.own_ref) | copy-start | bytes 2359300
  76.1 237.7 %copy-start.4 = (bf16[12,32,1024]{2,1,0:T(8,128)(2,1)}, bf16[12,32,1024]{2,1,0:T(8,128)(2,1)S(1)}, u32[]{:S(2)}) copy-start(bf16[12,32,1024]{2,1,0:T(8,128)(2,1)S(1)} %get-tuple-element.33.own_ref) | copy-start | bytes 2359300
  76.1 19.8 %collective-permute-start = (bf16[12,32,1024]{2,1,0:T(8,128)(2,1)}, bf16[12,32,1024]{2,1,0:T(8,128)(2,1)}, u32[]{:S(2)}, u32[]{:S(2)}) collective-permute-start(bf16[12,32,1024]{2,1,0:T(8,128)(2,1)} %get-tuple-element.42.own_ref), channel_id=1, source_target_pairs={{0,1},{3,2},{4,5},{7,6},{8,9},{11,10},{12,13},{15,14},{16,17},{19,... | collective-permute-start | bytes 2359304 | tf_op jit(solution)/shard_map/ppermute | solution.py:95
  95.9 11.0 %collective-permute-start.4 = (bf16[12,16,1024]{2,1,0:T(8,128)(2,1)S(1)}, bf16[12,16,1024]{2,1,0:T(8,128)(2,1)S(1)}, u32[]{:S(2)}, u32[]{:S(2)}) collective-permute-start(bf16[12,16,1024]{2,1,0:T(8,128)(2,1)S(1)} %pad_maximum_fusion.2), channel_id=1, source_target_pairs={{0,1},{3,2},{4,5},{7,6},{8,9},{11,10},{12,13},{15,14},{16,17},{19,... | collective-permute-start | bytes 1179656 | tf_op jit(solution)/shard_map/ppermute | solution.py:95
  121.7 31.8 %collective-permute-start.5 = (f32[8,32,1024]{2,1,0:T(8,128)}, f32[8,32,1024]{2,1,0:T(8,128)}, u32[]{:S(2)}, u32[]{:S(2)}) collective-permute-start(f32[8,32,1024]{2,1,0:T(8,128)} %shard_map.48), channel_id=1, source_target_pairs={{1,2},{2,1},{5,6},{6,5},{9,10},{10,9},{13,14},{14,13},{17,18},{18,... | collective-permute-start | bytes 3145736 | tf_op jit(solution)/shard_map/ppermute | solution.py:241
  123.4 20.4 %collective-permute-start.7 = (bf16[12,32,1024]{2,1,0:T(8,128)(2,1)}, bf16[12,32,1024]{2,1,0:T(8,128)(2,1)}, u32[]{:S(2)}, u32[]{:S(2)}) collective-permute-start(bf16[12,32,1024]{2,1,0:T(8,128)(2,1)} %get-tuple-element.21.own_ref), channel_id=1, source_target_pairs={{0,1},{3,2},{4,5},{7,6},{8,9},{11,10},{12,13},{15,14},{16,17},{19,... | collective-permute-start | bytes 2359304 | tf_op jit(solution)/shard_map/ppermute | solution.py:95
  153.6 29.5 %collective-permute-start.8 = (f32[8,32,1024]{2,1,0:T(8,128)}, f32[8,32,1024]{2,1,0:T(8,128)}, u32[]{:S(2)}, u32[]{:S(2)}) collective-permute-start(f32[8,32,1024]{2,1,0:T(8,128)} %shard_map.50), channel_id=1, source_target_pairs={{1,2},{2,1},{5,6},{6,5},{9,10},{10,9},{13,14},{14,13},{17,18},{18,... | collective-permute-start | bytes 3145736 | tf_op jit(solution)/shard_map/ppermute | solution.py:241
  155.2 18.1 %collective-permute-start.10 = (bf16[12,32,1024]{2,1,0:T(8,128)(2,1)}, bf16[12,32,1024]{2,1,0:T(8,128)(2,1)}, u32[]{:S(2)}, u32[]{:S(2)}) collective-permute-start(bf16[12,32,1024]{2,1,0:T(8,128)(2,1)} %get-tuple-element.23.own_ref), channel_id=1, source_target_pairs={{0,1},{3,2},{4,5},{7,6},{8,9},{11,10},{12,13},{15,14},{16,17},{19,... | collective-permute-start | bytes 2359304 | tf_op jit(solution)/shard_map/ppermute | solution.py:95
  183.1 29.4 %collective-permute-start.11 = (f32[8,32,1024]{2,1,0:T(8,128)}, f32[8,32,1024]{2,1,0:T(8,128)}, u32[]{:S(2)}, u32[]{:S(2)}) collective-permute-start(f32[8,32,1024]{2,1,0:T(8,128)} %shard_map.52), channel_id=1, source_target_pairs={{1,2},{2,1},{5,6},{6,5},{9,10},{10,9},{13,14},{14,13},{17,18},{18,... | collective-permute-start | bytes 3145736 | tf_op jit(solution)/shard_map/ppermute | solution.py:241
  184.7 18.0 %collective-permute-start.13 = (bf16[12,32,1024]{2,1,0:T(8,128)(2,1)}, bf16[12,32,1024]{2,1,0:T(8,128)(2,1)}, u32[]{:S(2)}, u32[]{:S(2)}) collective-permute-start(bf16[12,32,1024]{2,1,0:T(8,128)(2,1)} %get-tuple-element.25.own_ref), channel_id=1, source_target_pairs={{0,1},{3,2},{4,5},{7,6},{8,9},{11,10},{12,13},{15,14},{16,17},{19,... | collective-permute-start | bytes 2359304 | tf_op jit(solution)/shard_map/ppermute | solution.py:95
  212.5 26.8 %collective-permute-start.14 = (f32[8,32,1024]{2,1,0:T(8,128)}, f32[8,32,1024]{2,1,0:T(8,128)}, u32[]{:S(2)}, u32[]{:S(2)}) collective-permute-start(f32[8,32,1024]{2,1,0:T(8,128)} %shard_map.54), channel_id=1, source_target_pairs={{1,2},{2,1},{5,6},{6,5},{9,10},{10,9},{13,14},{14,13},{17,18},{18,... | collective-permute-start | bytes 3145736 | tf_op jit(solution)/shard_map/ppermute | solution.py:241
  214.1 15.4 %collective-permute-start.16 = (bf16[12,32,1024]{2,1,0:T(8,128)(2,1)S(1)}, bf16[12,32,1024]{2,1,0:T(8,128)(2,1)}, u32[]{:S(2)}, u32[]{:S(2)}) collective-permute-start(bf16[12,32,1024]{2,1,0:T(8,128)(2,1)S(1)} %get-tuple-element.27.own_ref), channel_id=1, source_target_pairs={{0,1},{3,2},{4,5},{7,6},{8,9},{11,10},{12,13},{15,14},{16,17},{19,... | collective-permute-start | bytes 2359304 | tf_op jit(solution)/shard_map/ppermute | solution.py:95
  239.3 28.1 %collective-permute-start.17 = (f32[8,32,1024]{2,1,0:T(8,128)}, f32[8,32,1024]{2,1,0:T(8,128)}, u32[]{:S(2)}, u32[]{:S(2)}) collective-permute-start(f32[8,32,1024]{2,1,0:T(8,128)} %shard_map.56), channel_id=1, source_target_pairs={{1,2},{2,1},{5,6},{6,5},{9,10},{10,9},{13,14},{14,13},{17,18},{18,... | collective-permute-start | bytes 3145736 | tf_op jit(solution)/shard_map/ppermute | solution.py:241
  241.0 15.8 %collective-permute-start.19 = (bf16[12,32,1024]{2,1,0:T(8,128)(2,1)S(1)}, bf16[12,32,1024]{2,1,0:T(8,128)(2,1)S(1)}, u32[]{:S(2)}, u32[]{:S(2)}) collective-permute-start(bf16[12,32,1024]{2,1,0:T(8,128)(2,1)S(1)} %get-tuple-element.29.own_ref), channel_id=1, source_target_pairs={{0,1},{3,2},{4,5},{7,6},{8,9},{11,10},{12,13},{15,14},{16,17},{19,... | collective-permute-start | bytes 2359304 | tf_op jit(solution)/shard_map/ppermute | solution.py:95
  267.4 27.1 %collective-permute-start.20 = (f32[8,32,1024]{2,1,0:T(8,128)}, f32[8,32,1024]{2,1,0:T(8,128)}, u32[]{:S(2)}, u32[]{:S(2)}) collective-permute-start(f32[8,32,1024]{2,1,0:T(8,128)} %shard_map.58), channel_id=1, source_target_pairs={{1,2},{2,1},{5,6},{6,5},{9,10},{10,9},{13,14},{14,13},{17,18},{18,... | collective-permute-start | bytes 3145736 | tf_op jit(solution)/shard_map/ppermute | solution.py:241
  269.0 27.1 %copy-start.22 = (f32[12,8,1024]{2,1,0:T(8,128)S(1)}, f32[12,8,1024]{2,1,0:T(8,128)}, u32[]{:S(2)}) copy-start(f32[12,8,1024]{2,1,0:T(8,128)} %get-tuple-element.50) | copy-start | bytes 1179652
  269.0 14.7 %collective-permute-start.22 = (bf16[12,32,1024]{2,1,0:T(8,128)(2,1)S(1)}, bf16[12,32,1024]{2,1,0:T(8,128)(2,1)S(1)}, u32[]{:S(2)}, u32[]{:S(2)}) collective-permute-start(bf16[12,32,1024]{2,1,0:T(8,128)(2,1)S(1)} %get-tuple-element.31.own_ref), channel_id=1, source_target_pairs={{0,1},{3,2},{4,5},{7,6},{8,9},{11,10},{12,13},{15,14},{16,17},{19,... | collective-permute-start | bytes 2359304 | tf_op jit(solution)/shard_map/ppermute | solution.py:95
  294.5 92.3 %collective-permute-start.23 = (f32[8,32,1024]{2,1,0:T(8,128)}, f32[8,32,1024]{2,1,0:T(8,128)}, u32[]{:S(2)}, u32[]{:S(2)}) collective-permute-start(f32[8,32,1024]{2,1,0:T(8,128)} %shard_map.60), channel_id=1, source_target_pairs={{1,2},{2,1},{5,6},{6,5},{9,10},{10,9},{13,14},{14,13},{17,18},{18,... | collective-permute-start | bytes 3145736 | tf_op jit(solution)/shard_map/ppermute | solution.py:241
  311.6 9.4 %copy-start.14 = (f32[8,32,1024]{2,1,0:T(8,128)}, f32[8,32,1024]{2,1,0:T(8,128)S(1)}, u32[]{:S(2)}) copy-start(f32[8,32,1024]{2,1,0:T(8,128)S(1)} %add.106) | copy-start | bytes 3145732
  312.6 46.6 %collective-permute-start.6 = (f32[4,32,1024]{2,1,0:T(8,128)}, f32[4,32,1024]{2,1,0:T(8,128)S(1)}, u32[]{:S(2)}, u32[]{:S(2)}) collective-permute-start(f32[4,32,1024]{2,1,0:T(8,128)} %slice.163), channel_id=1, source_target_pairs={{1,0},{2,3},{5,4},{6,7},{9,8},{10,11},{13,12},{14,15},{17,16},{18,... | collective-permute-start | bytes 1572872 | tf_op jit(solution)/shard_map/ppermute | solution.py:244
  313.9 63.1 %collective-permute-start.25 = (bf16[12,32,1024]{2,1,0:T(8,128)(2,1)S(1)}, bf16[12,32,1024]{2,1,0:T(8,128)(2,1)}, u32[]{:S(2)}, u32[]{:S(2)}) collective-permute-start(bf16[12,32,1024]{2,1,0:T(8,128)(2,1)S(1)} %get-tuple-element.33.own_ref), channel_id=1, source_target_pairs={{0,1},{3,2},{4,5},{7,6},{8,9},{11,10},{12,13},{15,14},{16,17},{19,... | collective-permute-start | bytes 2359304 | tf_op jit(solution)/shard_map/ppermute | solution.py:95
  332.5 1.2 copy-start.13
  333.6 54.7 %collective-permute-start.9 = (f32[4,32,1024]{2,1,0:T(8,128)}, f32[4,32,1024]{2,1,0:T(8,128)}, u32[]{:S(2)}, u32[]{:S(2)}) collective-permute-start(f32[4,32,1024]{2,1,0:T(8,128)} %slice.166), channel_id=1, source_target_pairs={{1,0},{2,3},{5,4},{6,7},{9,8},{10,11},{13,12},{14,15},{17,16},{18,... | collective-permute-start | bytes 1572872 | tf_op jit(solution)/shard_map/ppermute | solution.py:244
  354.1 5.0 %copy-start = (f32[512,1024]{1,0:T(8,128)S(1)}, f32[512,1024]{1,0:T(8,128)}, u32[]{:S(2)}) copy-start(f32[512,1024]{1,0:T(8,128)} %get-tuple-element.64) | copy-start | bytes 6291460
  354.1 5.0 %copy-start.15 = (f32[8,32,1024]{2,1,0:T(8,128)S(1)}, f32[8,32,1024]{2,1,0:T(8,128)}, u32[]{:S(2)}) copy-start(f32[8,32,1024]{2,1,0:T(8,128)} %copy-done.14) | copy-start | bytes 3145732
  357.8 50.4 %collective-permute-start.12 = (f32[4,32,1024]{2,1,0:T(8,128)}, f32[4,32,1024]{2,1,0:T(8,128)}, u32[]{:S(2)}, u32[]{:S(2)}) collective-permute-start(f32[4,32,1024]{2,1,0:T(8,128)} %slice.169), channel_id=1, source_target_pairs={{1,0},{2,3},{5,4},{6,7},{9,8},{10,11},{13,12},{14,15},{17,16},{18,... | collective-permute-start | bytes 1572872 | tf_op jit(solution)/shard_map/ppermute | solution.py:244
  375.7 61.7 %collective-permute-start.15 = (f32[4,32,1024]{2,1,0:T(8,128)}, f32[4,32,1024]{2,1,0:T(8,128)S(1)}, u32[]{:S(2)}, u32[]{:S(2)}) collective-permute-start(f32[4,32,1024]{2,1,0:T(8,128)} %slice.172), channel_id=1, source_target_pairs={{1,0},{2,3},{5,4},{6,7},{9,8},{10,11},{13,12},{14,15},{17,16},{18,... | collective-permute-start | bytes 1572872 | tf_op jit(solution)/shard_map/ppermute | solution.py:244
  386.7 70.2 %collective-permute-start.26 = (f32[8,32,1024]{2,1,0:T(8,128)}, f32[8,32,1024]{2,1,0:T(8,128)}, u32[]{:S(2)}, u32[]{:S(2)}) collective-permute-start(f32[8,32,1024]{2,1,0:T(8,128)} %shard_map.62), channel_id=1, source_target_pairs={{1,2},{2,1},{5,6},{6,5},{9,10},{10,9},{13,14},{14,13},{17,18},{18,... | collective-permute-start | bytes 3145736 | tf_op jit(solution)/shard_map/ppermute | solution.py:241
  403.3 5.0 %copy-start.1 = (f32[512,1024]{1,0:T(8,128)S(1)}, f32[512,1024]{1,0:T(8,128)}, u32[]{:S(2)}) copy-start(f32[512,1024]{1,0:T(8,128)} %get-tuple-element.64) | copy-start | bytes 6291460
  403.3 5.0 %copy-start.12 = (f32[8,32,1024]{2,1,0:T(8,128)S(1)}, f32[8,32,1024]{2,1,0:T(8,128)}, u32[]{:S(2)}) copy-start(f32[8,32,1024]{2,1,0:T(8,128)} %copy-done.11) | copy-start | bytes 3145732
  405.1 1.0 copy-start.16
  407.0 46.7 %collective-permute-start.18 = (f32[4,32,1024]{2,1,0:T(8,128)}, f32[4,32,1024]{2,1,0:T(8,128)S(1)}, u32[]{:S(2)}, u32[]{:S(2)}) collective-permute-start(f32[4,32,1024]{2,1,0:T(8,128)} %slice.175), channel_id=1, source_target_pairs={{1,0},{2,3},{5,4},{6,7},{9,8},{10,11},{13,12},{14,15},{17,16},{18,... | collective-permute-start | bytes 1572872 | tf_op jit(solution)/shard_map/ppermute | solution.py:244
  432.1 5.2 %copy-start.2 = (f32[512,1024]{1,0:T(8,128)S(1)}, f32[512,1024]{1,0:T(8,128)}, u32[]{:S(2)}) copy-start(f32[512,1024]{1,0:T(8,128)} %get-tuple-element.64) | copy-start | bytes 6291460
  432.1 5.2 %copy-start.10 = (f32[8,32,1024]{2,1,0:T(8,128)S(1)}, f32[8,32,1024]{2,1,0:T(8,128)}, u32[]{:S(2)}) copy-start(f32[8,32,1024]{2,1,0:T(8,128)} %copy-done.9) | copy-start | bytes 3145732
  435.8 24.2 %collective-permute-start.21 = (f32[4,32,1024]{2,1,0:T(8,128)}, f32[4,32,1024]{2,1,0:T(8,128)}, u32[]{:S(2)}, u32[]{:S(2)}) collective-permute-start(f32[4,32,1024]{2,1,0:T(8,128)} %slice.178), channel_id=1, source_target_pairs={{1,0},{2,3},{5,4},{6,7},{9,8},{10,11},{13,12},{14,15},{17,16},{18,... | collective-permute-start | bytes 1572872 | tf_op jit(solution)/shard_map/ppermute | solution.py:244
  450.4 3.3 copy-start.3
  450.4 3.4 copy-start.17
  452.2 4.7 copy-start.8
  452.3 13.0 %collective-permute-start.24 = (f32[4,32,1024]{2,1,0:T(8,128)S(1)}, f32[4,32,1024]{2,1,0:T(8,128)S(1)}, u32[]{:S(2)}, u32[]{:S(2)}) collective-permute-start(f32[4,32,1024]{2,1,0:T(8,128)S(1)} %slice.181), channel_id=1, source_target_pairs={{1,0},{2,3},{5,4},{6,7},{9,8},{10,11},{13,12},{14,15},{17,16},{18,... | collective-permute-start | bytes 1572872 | tf_op jit(solution)/shard_map/ppermute | solution.py:244
  456.9 3.1 copy-start.19
  458.4 12.7 %collective-permute-start.27 = (f32[4,32,1024]{2,1,0:T(8,128)S(1)}, f32[4,32,1024]{2,1,0:T(8,128)S(1)}, u32[]{:S(2)}, u32[]{:S(2)}) collective-permute-start(f32[4,32,1024]{2,1,0:T(8,128)S(1)} %slice.184), channel_id=1, source_target_pairs={{1,0},{2,3},{5,4},{6,7},{9,8},{10,11},{13,12},{14,15},{17,16},{18,... | collective-permute-start | bytes 1572872 | tf_op jit(solution)/shard_map/ppermute | solution.py:244
  (5 other events, 4.7 us)

commit v2 on v1

--- a/solution.py
+++ b/solution.py
@@ -122,9 +122,9 @@
 ROWS = 8
 
 
-def cross_kernel(own_ref, edge_ref, own_src_ref, edge_src_ref, out_ref):
+def cross_kernel(own_ref, src_ref, out_ref):
     segments = own_ref.shape[0]
-    sources = own_src_ref.shape[1]
+    sources = src_ref.shape[1]
     rows = own_ref.shape[1]
     bins = own_ref.shape[-1] // 2
 
@@ -132,9 +132,9 @@
         re_lanes = pl.ds(pl.multiple_of(tile * LANES, LANES), LANES)
         im_lanes = pl.ds(pl.multiple_of(bins + tile * LANES, LANES), LANES)
 
-        def step(m, acc, data_ref, src_ref):
-            wr = data_ref[m, :, re_lanes].astype(jnp.float32)
-            wi = data_ref[m, :, im_lanes].astype(jnp.float32)
+        def step(m, acc):
+            wr = own_ref[m, :, re_lanes].astype(jnp.float32)
+            wi = own_ref[m, :, im_lanes].astype(jnp.float32)
             out = []
             for j in range(sources):
                 sr = jnp.concatenate([src_ref[m, j, :, re_lanes]] * (rows // ROWS), axis=0)
@@ -144,8 +144,7 @@
             return tuple(out)
 
         acc = tuple(jnp.zeros((rows, LANES), jnp.float32) for _ in range(2 * sources))
-        acc = lax.fori_loop(0, segments, lambda m, a: step(m, a, own_ref, own_src_ref), acc)
-        acc = lax.fori_loop(0, segments, lambda m, a: step(m, a, edge_ref, edge_src_ref), acc)
+        acc = lax.fori_loop(0, segments, step, acc)
         for j in range(sources):
             out_ref[j, :, re_lanes] = acc[2 * j]
             out_ref[j, :, im_lanes] = acc[2 * j + 1]
@@ -154,22 +153,20 @@
     lax.fori_loop(0, bins // LANES, tile_body, 0)
 
 
-def cross_chunk(own, edge, own_src, edge_src):
+def cross_chunk(own, src):
     segments, width, length = own.shape
-    sources = own_src.shape[1]
+    sources = src.shape[1]
     step_rows = 2 * ROWS
     return pl.pallas_call(
         cross_kernel,
         grid=(width // step_rows,),
         in_specs=[
             pl.BlockSpec((segments, step_rows, length), lambda i: (0, i, 0)),
-            pl.BlockSpec((segments, step_rows, length), lambda i: (0, i, 0)),
-            pl.BlockSpec((segments, sources, ROWS, length), lambda i: (0, 0, 0, 0)),
             pl.BlockSpec((segments, sources, ROWS, length), lambda i: (0, 0, 0, 0)),
         ],
         out_specs=pl.BlockSpec((sources, step_rows, length), lambda i: (0, i, 0)),
         out_shape=jax.ShapeDtypeStruct((sources, width, length), jnp.float32),
-    )(own, edge, own_src, edge_src)
+    )(own, src)
 
 
 def butterfly_sum(values, axis):
@@ -219,30 +216,28 @@
     near = jnp.where(first_half, sources[:, :half], turned)
     inverse = inverse_table(length, 1.0 / math.sqrt(bins * seg_count * groups))
     is_edge = jnp.logical_or(place == 0, place == groups - 1)
-    edge_chunks = [edge_first(whitened[0], groups)]
-    pair = jnp.concatenate([far, near], axis=1)
-    pair, _ = lax.optimization_barrier((pair, edge_chunks[0]))
-    edge_pair = edge_first(pair, groups)
-    far_wide, edge_far_wide = widen(far, length), widen(edge_pair[:, :half], length)
-    near_wide, edge_near_wide = widen(near, length), widen(edge_pair[:, half:], length)
-    previous = edge_pair
-    for chunk in range(1, chunks):
-        own, _ = lax.optimization_barrier((whitened[chunk], previous))
-        previous = edge_first(own, groups)
-        edge_chunks.append(previous)
+    far_wide, near_wide = widen(far, length), widen(near, length)
     outs = []
-    last_sent = None
+    last_edge = None
+    last_middle = None
     for chunk in range(chunks):
         own = whitened[chunk]
-        edge_rows = edge_chunks[chunk]
-        far_part = cross_chunk(own, edge_rows, far_wide, edge_far_wide)
-        if last_sent is not None:
-            far_part, _ = lax.optimization_barrier((far_part, last_sent))
-        got = lax.ppermute(far_part, "tm", [(1, 2), (2, 1)])
-        last_sent = got
-        total = cross_chunk(own, edge_rows, near_wide, edge_near_wide) + got
-        back = lax.ppermute(total[:per_group], "tm", [(1, 0), (2, 3)])
-        final = jnp.where(is_edge, back, total[per_group:])
+        far_part = cross_chunk(own, far_wide)
+        near_part = cross_chunk(own, near_wide)
+        edge_out = jnp.concatenate([far_part, near_part[per_group:]], axis=0).astype(jnp.bfloat16)
+        if last_edge is not None:
+            edge_out, _ = lax.optimization_barrier((edge_out, last_edge))
+        edge_in = edge_first(edge_out, groups)
+        last_edge = edge_in
+        far_total = far_part + edge_in[:half].astype(jnp.float32)
+        if last_middle is not None:
+            far_total, _ = lax.optimization_barrier((far_total, last_middle))
+        got = lax.ppermute(far_total, "tm", [(1, 2), (2, 1)])
+        last_middle = got
+        low = near_part[:per_group] + got[:per_group]
+        high = near_part[per_group:] + edge_in[half:].astype(jnp.float32) + got[per_group:]
+        back = lax.ppermute(low, "tm", [(1, 0), (2, 3)])
+        final = jnp.where(is_edge, near_part[:per_group] + back, high)
         outs.append(jnp.dot(final, inverse, precision=lax.Precision.HIGHEST))
     return jnp.concatenate(outs, axis=1)
 

time: 476 us -> 358 us (0.75)
  Pallas kernels: 172 us -> 111 us
  waiting for transfers between devices: 99.5 us -> 64.9 us
  starting transfers between devices: 83.4 us -> 68.3 us
  local copies, waits for them, and re-layouts: 36.3 us -> 28.2 us
    ppermute x9 -> x8, waiting for transfers between devices: 85 us -> 7.93 us  [edge_first(): return lax.ppermute(values, 'tm', [(0, 1), (groups - 1, groups - 2)])]
    pallas_call x16, Pallas kernels: 156 us -> 96.1 us  [cross_chunk(): pl.pallas_call(cross_kernel, grid=(width // step_rows,), in_specs=[pl.Blo...]
    ppermute x16, waiting for transfers between devices: 3.69 us -> 42.9 us  [the longest x8 42.9 us: on_line(): back = lax.ppermute(low, 'tm', [(1, 0), (2, 3)])]
    ppermute x9 -> x8, starting transfers between devices: 53.9 us -> 43.5 us  [edge_first(): return lax.ppermute(values, 'tm', [(0, 1), (groups - 1, groups - 2)])]
    unnamed x51 -> x47, local copies, waits for them, and re-layouts: 13.7 us -> 7.85 us
    another operation x1 -> x9, other arithmetic: 8.54 us -> 10.4 us
    add x8 -> x16, other arithmetic: 13.8 us -> 13.2 us  [the longest x8 9.45 us: on_line(): far_total = far_part + edge_in[:half].astype(jnp.float32)]
  transfers between devices with their start and end apart: 28 -> 27, of which waited for: 12 -> 14; matrix products, arithmetic and copies ran while one was open for 14% -> 17% of each run, Pallas kernels for 31% -> 24%
where the time goes in v2:
time: 358 us; the launch traced here: 356 us
  Pallas kernels  111 us (31%)
  starting transfers between devices  68.3 us (19%)
  waiting for transfers between devices  64.9 us (18%)
  other arithmetic  41.2 us (12%)
  local copies, waits for them, and re-layouts  28.2 us (8%)
  matrix products  25.8 us (7%)
  between operations  16.4 us (5%)
    pallas_call x16, Pallas kernels, cross_chunk(): pl.pallas_call(cross_kernel, grid=(width // step_rows,), in_specs=[pl.Blo...  96.1 us
    ppermute x8, starting transfers between devices, edge_first(): return lax.ppermute(values, 'tm', [(0, 1), (groups - 1, groups - 2)])  43.5 us
    ppermute x8, waiting for transfers between devices, on_line(): back = lax.ppermute(low, 'tm', [(1, 0), (2, 3)])  42.9 us
    dot_general x8, matrix products, on_line(): outs.append(jnp.dot(final, inverse, precision=lax.Precision.HIGHEST))  25.8 us
    pallas_call x1, Pallas kernels, whiten_segments(): pl.pallas_call(whiten_kernel, grid=(segments,), in_specs=[pl.BlockSpec((N...  15.2 us
    ppermute x3, waiting for transfers between devices, butterfly_sum(): lax.ppermute(values, axis, [(b, b ^ step) for b in range(count)])  14.1 us
    ppermute x8, starting transfers between devices, on_line(): back = lax.ppermute(low, 'tm', [(1, 0), (2, 3)])  10.5 us
    another operation x9, other arithmetic  10.4 us
  transfers between devices with their start and end apart: 27, of which 14 were waited for; matrix products, arithmetic and copies ran while one was open for 17% of the time, Pallas kernels for 24%

profile of v2, /device:TPU:0, one launch (start us, length us, event | category | flops | bytes accessed | tf_op | source)
XLA Modules:
  0.0 356.2 jit_solution(7723660358848688611)
XLA Ops:
  0.0 8.5 %negate_convert_fusion = (bf16[1024,512]{1,0:T(8,128)(2,1)S(1)}, bf16[1024,512]{1,0:T(8,128)(2,1)S(1)}) fusion(), kind=kLoop, calls=%fused_computation.18 | loop fusion | flops 8912896 | bytes 2097152 | tf_op jit(solution)/shard_map/convert.17
  22.2 7.6 %copy.7 = bf16[256,2,6,1024]{3,0,2,1:T(8,128)(2,1)} copy(bf16[256,2,6,1024]{3,1,2,0:T(2,128)(2,1)} %param.4) | data formatting | bytes 12582912 | tf_op args[0]
  36.4 15.2 %shard_map.46 = bf16[8,12,32,1024]{3,2,1,0:T(8,128)(2,1)} custom-call(bf16[12,256,1024]{2,1,0:T(8,128)(2,1)} %bitcast.50, bf16[1024,1024]{1,0:T(8,128)(2,1)} %pad_maximum_fusion.forward_ref, f32[12,256,1]{2,1,0:T(8,128)} %copy.9.mask_ref), custom_call_target="tpu_custom_call" | custom-call | tf_op jit(solution)/shard_map/pallas_call | solution.py:108
  55.7 2.9 collective-permute-start.1
  58.6 9.4 %collective-permute-done.1 = bf16[12,16,1024]{2,1,0:T(8,128)(2,1)S(1)} collective-permute-done((bf16[12,16,1024]{2,1,0:T(8,128)(2,1)S(1)}, bf16[12,16,1024]{2,1,0:T(8,128)(2,1)S(1)}, u32[]{:S(2)}, u32[]{:S(2)}) %collective-permute-start.1) | collective-permute-done | bytes 393248 | tf_op jit(solution)/shard_map/ppermute | solution.py:176
  70.0 5.5 %slice_bitcast_fusion = (bf16[12,32,1024]{2,1,0:T(8,128)(2,1)}, bf16[12,32,1024]{2,1,0:T(8,128)(2,1)}, bf16[12,32,1024]{2,1,0:T(8,128)(2,1)}, bf16[12,32,1024]{2...) fusion(bf16[8,12,32,1024]{3,2,1,0:T(8,128)(2,1)} %shard_map.46), kind=kLoop, calls=%fused_computation.40 | loop fusion | bytes 12582912 | tf_op jit(solution)/shard_map/squeeze | solution.py:224
  75.5 3.3 collective-permute-done.2
  81.3 6.0 %shard_map.48 = f32[8,32,1024]{2,1,0:T(8,128)} custom-call(bf16[12,32,1024]{2,1,0:T(8,128)(2,1)} %get-tuple-element.40.own_ref, f32[12,8,8,1024]{3,2,1,0:T(8,128)} %broadcast_in_dim.38.src_ref), custom_call_target="tpu_custom_call" | custom-call | tf_op jit(solution)/shard_map/pallas_call | solution.py:160
  89.3 6.0 %shard_map.47 = f32[8,32,1024]{2,1,0:T(8,128)} custom-call(bf16[12,32,1024]{2,1,0:T(8,128)(2,1)} %get-tuple-element.40.own_ref, f32[12,8,8,1024]{3,2,1,0:T(8,128)} %broadcast_in_dim.37.src_ref), custom_call_target="tpu_custom_call" | custom-call | tf_op jit(solution)/shard_map/pallas_call | solution.py:160
  97.4 4.3 %collective-permute-start.3 = (bf16[12,32,1024]{2,1,0:T(8,128)(2,1)}, bf16[12,32,1024]{2,1,0:T(8,128)(2,1)}, u32[]{:S(2)}, u32[]{:S(2)}) collective-permute-start(bf16[12,32,1024]{2,1,0:T(8,128)(2,1)} %pad_maximum_fusion.1), channel_id=1, source_target_pairs={{0,1},{3,2},{4,5},{7,6},{8,9},{11,10},{12,13},{15,14},{16,17},{19,... | collective-permute-start | bytes 2359304 | tf_op jit(solution)/shard_map/ppermute | solution.py:95
  101.8 6.0 %shard_map.50 = f32[8,32,1024]{2,1,0:T(8,128)} custom-call(bf16[12,32,1024]{2,1,0:T(8,128)(2,1)} %get-tuple-element.39.own_ref, f32[12,8,8,1024]{3,2,1,0:T(8,128)} %broadcast_in_dim.38.src_ref), custom_call_target="tpu_custom_call" | custom-call | tf_op jit(solution)/shard_map/pallas_call | solution.py:160
  107.7 6.1 %shard_map.49 = f32[8,32,1024]{2,1,0:T(8,128)} custom-call(bf16[12,32,1024]{2,1,0:T(8,128)(2,1)} %get-tuple-element.39.own_ref, f32[12,8,8,1024]{3,2,1,0:T(8,128)} %broadcast_in_dim.37.src_ref), custom_call_target="tpu_custom_call" | custom-call | tf_op jit(solution)/shard_map/pallas_call | solution.py:160
  116.5 5.3 %collective-permute-start.6 = (bf16[12,32,1024]{2,1,0:T(8,128)(2,1)S(1)}, bf16[12,32,1024]{2,1,0:T(8,128)(2,1)}, u32[]{:S(2)}, u32[]{:S(2)}) collective-permute-start(bf16[12,32,1024]{2,1,0:T(8,128)(2,1)S(1)} %pad_maximum_fusion.2), channel_id=1, source_target_pairs={{0,1},{3,2},{4,5},{7,6},{8,9},{11,10},{12,13},{15,14},{16,17},{19,... | collective-permute-start | bytes 2359304 | tf_op jit(solution)/shard_map/ppermute | solution.py:95
  125.6 6.0 %shard_map.52 = f32[8,32,1024]{2,1,0:T(8,128)} custom-call(bf16[12,32,1024]{2,1,0:T(8,128)(2,1)} %get-tuple-element.38.own_ref, f32[12,8,8,1024]{3,2,1,0:T(8,128)} %broadcast_in_dim.38.src_ref), custom_call_target="tpu_custom_call" | custom-call | tf_op jit(solution)/shard_map/pallas_call | solution.py:160
  131.6 6.0 %shard_map.51 = f32[8,32,1024]{2,1,0:T(8,128)} custom-call(bf16[12,32,1024]{2,1,0:T(8,128)(2,1)} %get-tuple-element.38.own_ref, f32[12,8,8,1024]{3,2,1,0:T(8,128)} %broadcast_in_dim.37.src_ref), custom_call_target="tpu_custom_call" | custom-call | tf_op jit(solution)/shard_map/pallas_call | solution.py:160
  139.8 3.1 collective-permute-start.9
  145.7 6.0 %shard_map.54 = f32[8,32,1024]{2,1,0:T(8,128)} custom-call(bf16[12,32,1024]{2,1,0:T(8,128)(2,1)} %get-tuple-element.37.own_ref, f32[12,8,8,1024]{3,2,1,0:T(8,128)} %broadcast_in_dim.38.src_ref), custom_call_target="tpu_custom_call" | custom-call | tf_op jit(solution)/shard_map/pallas_call | solution.py:160
  151.7 6.1 %shard_map.53 = f32[8,32,1024]{2,1,0:T(8,128)} custom-call(bf16[12,32,1024]{2,1,0:T(8,128)(2,1)} %get-tuple-element.37.own_ref, f32[12,8,8,1024]{3,2,1,0:T(8,128)} %broadcast_in_dim.37.src_ref), custom_call_target="tpu_custom_call" | custom-call | tf_op jit(solution)/shard_map/pallas_call | solution.py:160
  160.0 7.8 %collective-permute-start.12 = (bf16[12,32,1024]{2,1,0:T(8,128)(2,1)}, bf16[12,32,1024]{2,1,0:T(8,128)(2,1)}, u32[]{:S(2)}, u32[]{:S(2)}) collective-permute-start(bf16[12,32,1024]{2,1,0:T(8,128)(2,1)} %pad_maximum_fusion.4), channel_id=1, source_target_pairs={{0,1},{3,2},{4,5},{7,6},{8,9},{11,10},{12,13},{15,14},{16,17},{19,... | collective-permute-start | bytes 2359304 | tf_op jit(solution)/shard_map/ppermute | solution.py:95
  167.7 2.1 convert_add_fusion.5
  170.6 6.0 %shard_map.56 = f32[8,32,1024]{2,1,0:T(8,128)} custom-call(bf16[12,32,1024]{2,1,0:T(8,128)(2,1)} %get-tuple-element.36.own_ref, f32[12,8,8,1024]{3,2,1,0:T(8,128)} %broadcast_in_dim.38.src_ref), custom_call_target="tpu_custom_call" | custom-call | tf_op jit(solution)/shard_map/pallas_call | solution.py:160
  176.6 6.1 %shard_map.55 = f32[8,32,1024]{2,1,0:T(8,128)} custom-call(bf16[12,32,1024]{2,1,0:T(8,128)(2,1)} %get-tuple-element.36.own_ref, f32[12,8,8,1024]{3,2,1,0:T(8,128)} %broadcast_in_dim.37.src_ref), custom_call_target="tpu_custom_call" | custom-call | tf_op jit(solution)/shard_map/pallas_call | solution.py:160
  184.8 6.5 %collective-permute-start.15 = (bf16[12,32,1024]{2,1,0:T(8,128)(2,1)}, bf16[12,32,1024]{2,1,0:T(8,128)(2,1)}, u32[]{:S(2)}, u32[]{:S(2)}) collective-permute-start(bf16[12,32,1024]{2,1,0:T(8,128)(2,1)} %pad_maximum_fusion.5), channel_id=1, source_target_pairs={{0,1},{3,2},{4,5},{7,6},{8,9},{11,10},{12,13},{15,14},{16,17},{19,... | collective-permute-start | bytes 2359304 | tf_op jit(solution)/shard_map/ppermute | solution.py:95
  191.3 2.2 convert_add_fusion.4
  195.1 9.2 %sine_multiply_fusion = (f32[512,1024]{1,0:T(8,128)S(1)}, f32[512,1024]{1,0:T(8,128)}) fusion(f32[512]{0:T(512)S(1)} %fusion.84, f32[512]{0:T(512)S(1)} %select_multiply_fusion), kind=kLoop, calls=%fused_computation.14 | loop fusion | flops 8388608 | bytes 4198400 | tf_op jit(solution)/shard_map/mul | solution.py:35
  204.4 6.0 %shard_map.58 = f32[8,32,1024]{2,1,0:T(8,128)} custom-call(bf16[12,32,1024]{2,1,0:T(8,128)(2,1)} %get-tuple-element.35.own_ref, f32[12,8,8,1024]{3,2,1,0:T(8,128)} %broadcast_in_dim.38.src_ref), custom_call_target="tpu_custom_call" | custom-call | tf_op jit(solution)/shard_map/pallas_call | solution.py:160
  210.3 6.0 %shard_map.57 = f32[8,32,1024]{2,1,0:T(8,128)} custom-call(bf16[12,32,1024]{2,1,0:T(8,128)(2,1)} %get-tuple-element.35.own_ref, f32[12,8,8,1024]{3,2,1,0:T(8,128)} %broadcast_in_dim.37.src_ref), custom_call_target="tpu_custom_call" | custom-call | tf_op jit(solution)/shard_map/pallas_call | solution.py:160
  216.3 6.0 %shard_map.60 = f32[8,32,1024]{2,1,0:T(8,128)} custom-call(bf16[12,32,1024]{2,1,0:T(8,128)(2,1)} %get-tuple-element.34.own_ref, f32[12,8,8,1024]{3,2,1,0:T(8,128)} %broadcast_in_dim.38.src_ref), custom_call_target="tpu_custom_call" | custom-call | tf_op jit(solution)/shard_map/pallas_call | solution.py:160
  222.3 6.0 %shard_map.59 = f32[8,32,1024]{2,1,0:T(8,128)} custom-call(bf16[12,32,1024]{2,1,0:T(8,128)(2,1)} %get-tuple-element.34.own_ref, f32[12,8,8,1024]{3,2,1,0:T(8,128)} %broadcast_in_dim.37.src_ref), custom_call_target="tpu_custom_call" | custom-call | tf_op jit(solution)/shard_map/pallas_call | solution.py:160
  228.3 6.0 %shard_map.62 = f32[8,32,1024]{2,1,0:T(8,128)} custom-call(bf16[12,32,1024]{2,1,0:T(8,128)(2,1)} %get-tuple-element.33.own_ref, f32[12,8,8,1024]{3,2,1,0:T(8,128)} %broadcast_in_dim.38.src_ref), custom_call_target="tpu_custom_call" | custom-call | tf_op jit(solution)/shard_map/pallas_call | solution.py:160
  234.3 6.0 %shard_map.61 = f32[8,32,1024]{2,1,0:T(8,128)} custom-call(bf16[12,32,1024]{2,1,0:T(8,128)(2,1)} %get-tuple-element.33.own_ref, f32[12,8,8,1024]{3,2,1,0:T(8,128)} %broadcast_in_dim.37.src_ref), custom_call_target="tpu_custom_call" | custom-call | tf_op jit(solution)/shard_map/pallas_call | solution.py:160
  244.3 4.6 %collective-permute-start.18 = (bf16[12,32,1024]{2,1,0:T(8,128)(2,1)S(1)}, bf16[12,32,1024]{2,1,0:T(8,128)(2,1)S(1)}, u32[]{:S(2)}, u32[]{:S(2)}) collective-permute-start(bf16[12,32,1024]{2,1,0:T(8,128)(2,1)S(1)} %pad_maximum_fusion.6), channel_id=1, source_target_pairs={{0,1},{3,2},{4,5},{7,6},{8,9},{11,10},{12,13},{15,14},{16,17},{19,... | collective-permute-start | bytes 2359304 | tf_op jit(solution)/shard_map/ppermute | solution.py:95
  256.4 5.8 %collective-permute-done.18 = bf16[12,32,1024]{2,1,0:T(8,128)(2,1)S(1)} collective-permute-done((bf16[12,32,1024]{2,1,0:T(8,128)(2,1)S(1)}, bf16[12,32,1024]{2,1,0:T(8,128)(2,1)S(1)}, u32[]{:S(2)}, u32[]{:S(2)}) %collective-permute-start.18) | collective-permute-done | bytes 786464 | tf_op jit(solution)/shard_map/ppermute | solution.py:95
  262.1 4.4 %collective-permute-start.21 = (bf16[12,32,1024]{2,1,0:T(8,128)(2,1)S(1)}, bf16[12,32,1024]{2,1,0:T(8,128)(2,1)S(1)}, u32[]{:S(2)}, u32[]{:S(2)}) collective-permute-start(bf16[12,32,1024]{2,1,0:T(8,128)(2,1)S(1)} %pad_maximum_fusion.7), channel_id=1, source_target_pairs={{0,1},{3,2},{4,5},{7,6},{8,9},{11,10},{12,13},{15,14},{16,17},{19,... | collective-permute-start | bytes 2359304 | tf_op jit(solution)/shard_map/ppermute | solution.py:95
  267.6 3.7 %convolution_dynamic-update-slice_fusion.7 = f32[4,256,1024]{2,1,0:T(8,128)S(1)} fusion(f32[8,32,1024]{2,1,0:T(8,128)} %collective-permute-done.4, f32[4,32,1024]{2,1,0:T(8,128)S(1)} %collective-permute-done.5, f32[8,32,1024]{2,1,0:T(8,128)S(1)} %copy-done.13, bf16[12,32,1024]{2,1,0:T(8,128)(2,1)} %collective-permute-done.3, pred[]{:T(512)S(6)} %or.3, ...), kind=kOutput, calls=%fused_computation.31 | convolution fusion | flops 1612316672 | bytes 7077889 | tf_op jit(solution)/shard_map/dot_general | solution.py:241
  272.7 2.2 collective-permute-done.8
  274.9 3.6 %convolution_dynamic-update-slice_fusion.6 = f32[4,256,1024]{2,1,0:T(8,128)S(1)} fusion(f32[4,256,1024]{2,1,0:T(8,128)S(1)} %convolution_dynamic-update-slice_fusion.7, f32[8,32,1024]{2,1,0:T(8,128)} %collective-permute-done.7, f32[4,32,1024]{2,1,0:T(8,128)S(1)} %collective-permute-done.8, f32[8,32,1024]{2,1,0:T(8,128)S(1)} %copy-done.12, ...), kind=kOutput, calls=%fused_computation.30 | convolution fusion | flops 1612316672 | bytes 7077889 | tf_op jit(solution)/shard_map/dot_general | solution.py:241
  278.5 7.6 %collective-permute-start.24 = (bf16[12,32,1024]{2,1,0:T(8,128)(2,1)S(1)}, bf16[12,32,1024]{2,1,0:T(8,128)(2,1)S(1)}, u32[]{:S(2)}, u32[]{:S(2)}) collective-permute-start(bf16[12,32,1024]{2,1,0:T(8,128)(2,1)S(1)} %pad_maximum_fusion.8), channel_id=1, source_target_pairs={{0,1},{3,2},{4,5},{7,6},{8,9},{11,10},{12,13},{15,14},{16,17},{19,... | collective-permute-start | bytes 2359304 | tf_op jit(solution)/shard_map/ppermute | solution.py:95
  287.6 3.4 convolution_dynamic-update-slice_fusion.5
  296.6 15.0 %collective-permute-done.14 = f32[4,32,1024]{2,1,0:T(8,128)S(1)} collective-permute-done((f32[4,32,1024]{2,1,0:T(8,128)S(1)}, f32[4,32,1024]{2,1,0:T(8,128)S(1)}, u32[]{:S(2)}, u32[]{:S(2)}) %collective-permute-start.14) | collective-permute-done | bytes 524320 | tf_op jit(solution)/shard_map/ppermute | solution.py:239
  311.6 3.6 %convolution_dynamic-update-slice_fusion.4 = f32[4,256,1024]{2,1,0:T(8,128)S(1)} fusion(f32[4,256,1024]{2,1,0:T(8,128)S(1)} %convolution_dynamic-update-slice_fusion.5, f32[8,32,1024]{2,1,0:T(8,128)} %collective-permute-done.13, f32[4,32,1024]{2,1,0:T(8,128)S(1)} %collective-permute-done.14, f32[8,32,1024]{2,1,0:T(8,128)S(1)} %copy-done.9, ...), kind=kOutput, calls=%fused_computation.28 | convolution fusion | flops 1612316672 | bytes 7077889 | tf_op jit(solution)/shard_map/dot_general | solution.py:241
  317.2 3.4 convolution_dynamic-update-slice_fusion.3
  324.8 16.9 %collective-permute-done.20 = f32[4,32,1024]{2,1,0:T(8,128)S(1)} collective-permute-done((f32[4,32,1024]{2,1,0:T(8,128)S(1)}, f32[4,32,1024]{2,1,0:T(8,128)S(1)}, u32[]{:S(2)}, u32[]{:S(2)}) %collective-permute-start.20) | collective-permute-done | bytes 524320 | tf_op jit(solution)/shard_map/ppermute | solution.py:239
  341.7 2.4 convolution_dynamic-update-slice_fusion.2
  344.1 3.2 collective-permute-done.23
  347.3 2.4 convolution_dynamic-update-slice_fusion.1
  349.7 3.2 collective-permute-done.26
  352.9 3.3 convolution_dynamic-update-slice_fusion
  (139 shorter events, 62.1 us)
Async XLA Ops:
  0.0 8.6 %copy-start.21 = (s32[4]{0:T(128)S(1)}, s32[4]{0:T(128)}, u32[]{:S(2)}) copy-start(s32[4]{0:T(128)} %param.7) | copy-start | bytes 52
  22.2 7.6 %copy-start.20 = (s32[256,2,6]{0,1,2:T(2,128)S(1)}, s32[256,2,6]{0,1,2:T(2,128)}, u32[]{:S(2)}) copy-start(s32[256,2,6]{0,1,2:T(2,128)} %param.5) | copy-start | bytes 36868
  22.2 9.3 %copy-start.22 = (s32[4]{0:T(128)S(1)}, s32[4]{0:T(128)}, u32[]{:S(2)}) copy-start(s32[4]{0:T(128)} %param.6) | copy-start | bytes 52
  53.5 1.9 collective-permute-start
  55.7 12.3 %collective-permute-start.1 = (bf16[12,16,1024]{2,1,0:T(8,128)(2,1)S(1)}, bf16[12,16,1024]{2,1,0:T(8,128)(2,1)S(1)}, u32[]{:S(2)}, u32[]{:S(2)}) collective-permute-start(bf16[12,16,1024]{2,1,0:T(8,128)(2,1)S(1)} %fusion.85), channel_id=1, source_target_pairs={{0,8},{4,12},{8,0},{12,4},{16,24},{20,28},{24,16},{28,20},{1,9},{5... | collective-permute-start | bytes 1179656 | tf_op jit(solution)/shard_map/ppermute | solution.py:176
  68.2 10.7 %collective-permute-start.2 = (bf16[12,16,1024]{2,1,0:T(8,128)(2,1)S(1)}, bf16[12,16,1024]{2,1,0:T(8,128)(2,1)S(1)}, u32[]{:S(2)}, u32[]{:S(2)}) collective-permute-start(bf16[12,16,1024]{2,1,0:T(8,128)(2,1)S(1)} %add.200), channel_id=1, source_target_pairs={{0,16},{4,20},{8,24},{12,28},{16,0},{20,4},{24,8},{28,12},{1,17},{... | collective-permute-start | bytes 1179656 | tf_op jit(solution)/shard_map/ppermute | solution.py:176
  89.3 7.1 %copy-start.8 = (f32[8,32,1024]{2,1,0:T(8,128)S(1)}, f32[8,32,1024]{2,1,0:T(8,128)}, u32[]{:S(2)}) copy-start(f32[8,32,1024]{2,1,0:T(8,128)} %shard_map.48) | copy-start | bytes 3145732
  97.4 19.1 %collective-permute-start.3 = (bf16[12,32,1024]{2,1,0:T(8,128)(2,1)}, bf16[12,32,1024]{2,1,0:T(8,128)(2,1)}, u32[]{:S(2)}, u32[]{:S(2)}) collective-permute-start(bf16[12,32,1024]{2,1,0:T(8,128)(2,1)} %pad_maximum_fusion.1), channel_id=1, source_target_pairs={{0,1},{3,2},{4,5},{7,6},{8,9},{11,10},{12,13},{15,14},{16,17},{19,... | collective-permute-start | bytes 2359304 | tf_op jit(solution)/shard_map/ppermute | solution.py:95
  107.7 7.1 %copy-start.7 = (f32[8,32,1024]{2,1,0:T(8,128)S(1)}, f32[8,32,1024]{2,1,0:T(8,128)}, u32[]{:S(2)}) copy-start(f32[8,32,1024]{2,1,0:T(8,128)} %shard_map.50) | copy-start | bytes 3145732
  116.5 23.3 %collective-permute-start.6 = (bf16[12,32,1024]{2,1,0:T(8,128)(2,1)S(1)}, bf16[12,32,1024]{2,1,0:T(8,128)(2,1)}, u32[]{:S(2)}, u32[]{:S(2)}) collective-permute-start(bf16[12,32,1024]{2,1,0:T(8,128)(2,1)S(1)} %pad_maximum_fusion.2), channel_id=1, source_target_pairs={{0,1},{3,2},{4,5},{7,6},{8,9},{11,10},{12,13},{15,14},{16,17},{19,... | collective-permute-start | bytes 2359304 | tf_op jit(solution)/shard_map/ppermute | solution.py:95
  123.9 20.2 %collective-permute-start.4 = (f32[8,32,1024]{2,1,0:T(8,128)}, f32[8,32,1024]{2,1,0:T(8,128)}, u32[]{:S(2)}, u32[]{:S(2)}) collective-permute-start(f32[8,32,1024]{2,1,0:T(8,128)} %convert_add_fusion.7), channel_id=1, source_target_pairs={{1,2},{2,1},{5,6},{6,5},{9,10},{10,9},{13,14},{14,13},{17,18},{18,... | collective-permute-start | bytes 3145736 | tf_op jit(solution)/shard_map/ppermute | solution.py:235
  131.6 7.1 %copy-start.5 = (f32[8,32,1024]{2,1,0:T(8,128)S(1)}, f32[8,32,1024]{2,1,0:T(8,128)}, u32[]{:S(2)}) copy-start(f32[8,32,1024]{2,1,0:T(8,128)} %shard_map.52) | copy-start | bytes 3145732
  139.8 20.2 %collective-permute-start.9 = (bf16[12,32,1024]{2,1,0:T(8,128)(2,1)}, bf16[12,32,1024]{2,1,0:T(8,128)(2,1)}, u32[]{:S(2)}, u32[]{:S(2)}) collective-permute-start(bf16[12,32,1024]{2,1,0:T(8,128)(2,1)} %pad_maximum_fusion.3), channel_id=1, source_target_pairs={{0,1},{3,2},{4,5},{7,6},{8,9},{11,10},{12,13},{15,14},{16,17},{19,... | collective-permute-start | bytes 2359304 | tf_op jit(solution)/shard_map/ppermute | solution.py:95
  144.1 25.8 %collective-permute-start.7 = (f32[8,32,1024]{2,1,0:T(8,128)S(1)}, f32[8,32,1024]{2,1,0:T(8,128)}, u32[]{:S(2)}, u32[]{:S(2)}) collective-permute-start(f32[8,32,1024]{2,1,0:T(8,128)S(1)} %convert_add_fusion.6), channel_id=1, source_target_pairs={{1,2},{2,1},{5,6},{6,5},{9,10},{10,9},{13,14},{14,13},{17,18},{18,... | collective-permute-start | bytes 3145736 | tf_op jit(solution)/shard_map/ppermute | solution.py:235
  151.7 7.1 %copy-start.6 = (f32[8,32,1024]{2,1,0:T(8,128)S(1)}, f32[8,32,1024]{2,1,0:T(8,128)}, u32[]{:S(2)}) copy-start(f32[8,32,1024]{2,1,0:T(8,128)} %shard_map.54) | copy-start | bytes 3145732
  160.0 24.9 %collective-permute-start.12 = (bf16[12,32,1024]{2,1,0:T(8,128)(2,1)}, bf16[12,32,1024]{2,1,0:T(8,128)(2,1)}, u32[]{:S(2)}, u32[]{:S(2)}) collective-permute-start(bf16[12,32,1024]{2,1,0:T(8,128)(2,1)} %pad_maximum_fusion.4), channel_id=1, source_target_pairs={{0,1},{3,2},{4,5},{7,6},{8,9},{11,10},{12,13},{15,14},{16,17},{19,... | collective-permute-start | bytes 2359304 | tf_op jit(solution)/shard_map/ppermute | solution.py:95
  169.9 23.6 %collective-permute-start.10 = (f32[8,32,1024]{2,1,0:T(8,128)}, f32[8,32,1024]{2,1,0:T(8,128)S(1)}, u32[]{:S(2)}, u32[]{:S(2)}) collective-permute-start(f32[8,32,1024]{2,1,0:T(8,128)} %convert_add_fusion.5), channel_id=1, source_target_pairs={{1,2},{2,1},{5,6},{6,5},{9,10},{10,9},{13,14},{14,13},{17,18},{18,... | collective-permute-start | bytes 3145736 | tf_op jit(solution)/shard_map/ppermute | solution.py:235
  176.6 7.2 %copy-start.3 = (f32[8,32,1024]{2,1,0:T(8,128)S(1)}, f32[8,32,1024]{2,1,0:T(8,128)}, u32[]{:S(2)}) copy-start(f32[8,32,1024]{2,1,0:T(8,128)} %shard_map.56) | copy-start | bytes 3145732
  184.8 59.4 %collective-permute-start.15 = (bf16[12,32,1024]{2,1,0:T(8,128)(2,1)}, bf16[12,32,1024]{2,1,0:T(8,128)(2,1)}, u32[]{:S(2)}, u32[]{:S(2)}) collective-permute-start(bf16[12,32,1024]{2,1,0:T(8,128)(2,1)} %pad_maximum_fusion.5), channel_id=1, source_target_pairs={{0,1},{3,2},{4,5},{7,6},{8,9},{11,10},{12,13},{15,14},{16,17},{19,... | collective-permute-start | bytes 2359304 | tf_op jit(solution)/shard_map/ppermute | solution.py:95
  193.5 56.6 %collective-permute-start.13 = (f32[8,32,1024]{2,1,0:T(8,128)}, f32[8,32,1024]{2,1,0:T(8,128)}, u32[]{:S(2)}, u32[]{:S(2)}) collective-permute-start(f32[8,32,1024]{2,1,0:T(8,128)} %convert_add_fusion.4), channel_id=1, source_target_pairs={{1,2},{2,1},{5,6},{6,5},{9,10},{10,9},{13,14},{14,13},{17,18},{18,... | collective-permute-start | bytes 3145736 | tf_op jit(solution)/shard_map/ppermute | solution.py:235
  240.2 3.7 %copy-start.2 = (f32[8,32,1024]{2,1,0:T(8,128)S(1)}, f32[8,32,1024]{2,1,0:T(8,128)}, u32[]{:S(2)}) copy-start(f32[8,32,1024]{2,1,0:T(8,128)} %shard_map.60) | copy-start | bytes 3145732
  240.2 3.8 %copy-start.11 = (f32[8,32,1024]{2,1,0:T(8,128)S(1)}, f32[8,32,1024]{2,1,0:T(8,128)}, u32[]{:S(2)}) copy-start(f32[8,32,1024]{2,1,0:T(8,128)} %shard_map.61) | copy-start | bytes 3145732
  241.5 2.6 copy-start.1
  244.3 17.9 %collective-permute-start.18 = (bf16[12,32,1024]{2,1,0:T(8,128)(2,1)S(1)}, bf16[12,32,1024]{2,1,0:T(8,128)(2,1)S(1)}, u32[]{:S(2)}, u32[]{:S(2)}) collective-permute-start(bf16[12,32,1024]{2,1,0:T(8,128)(2,1)S(1)} %pad_maximum_fusion.6), channel_id=1, source_target_pairs={{0,1},{3,2},{4,5},{7,6},{8,9},{11,10},{12,13},{15,14},{16,17},{19,... | collective-permute-start | bytes 2359304 | tf_op jit(solution)/shard_map/ppermute | solution.py:95
  250.1 3.8 %copy-start.12 = (f32[8,32,1024]{2,1,0:T(8,128)S(1)}, f32[8,32,1024]{2,1,0:T(8,128)}, u32[]{:S(2)}) copy-start(f32[8,32,1024]{2,1,0:T(8,128)} %shard_map.49) | copy-start | bytes 3145732
  250.1 16.6 %collective-permute-start.16 = (f32[8,32,1024]{2,1,0:T(8,128)S(1)}, f32[8,32,1024]{2,1,0:T(8,128)S(1)}, u32[]{:S(2)}, u32[]{:S(2)}) collective-permute-start(f32[8,32,1024]{2,1,0:T(8,128)S(1)} %convert_add_fusion.3), channel_id=1, source_target_pairs={{1,2},{2,1},{5,6},{6,5},{9,10},{10,9},{13,14},{14,13},{17,18},{18,... | collective-permute-start | bytes 3145736 | tf_op jit(solution)/shard_map/ppermute | solution.py:235
  251.1 15.5 %copy-start.4 = (f32[8,32,1024]{2,1,0:T(8,128)S(1)}, f32[8,32,1024]{2,1,0:T(8,128)}, u32[]{:S(2)}) copy-start(f32[8,32,1024]{2,1,0:T(8,128)} %shard_map.58) | copy-start | bytes 3145732
  252.5 15.1 %copy-start = (f32[512,1024]{1,0:T(8,128)S(1)}, f32[512,1024]{1,0:T(8,128)}, u32[]{:S(2)}) copy-start(f32[512,1024]{1,0:T(8,128)} %get-tuple-element.60) | copy-start | bytes 6291460
  252.5 15.1 %collective-permute-start.5 = (f32[4,32,1024]{2,1,0:T(8,128)S(1)}, f32[4,32,1024]{2,1,0:T(8,128)S(1)}, u32[]{:S(2)}, u32[]{:S(2)}) collective-permute-start(f32[4,32,1024]{2,1,0:T(8,128)S(1)} %slice_add_fusion.15), channel_id=1, source_target_pairs={{1,0},{2,3},{5,4},{6,7},{9,8},{10,11},{13,12},{14,15},{17,16},{18,... | collective-permute-start | bytes 1572872 | tf_op jit(solution)/shard_map/ppermute | solution.py:239
  255.1 19.8 %collective-permute-start.8 = (f32[4,32,1024]{2,1,0:T(8,128)S(1)}, f32[4,32,1024]{2,1,0:T(8,128)S(1)}, u32[]{:S(2)}, u32[]{:S(2)}) collective-permute-start(f32[4,32,1024]{2,1,0:T(8,128)S(1)} %slice_add_fusion.13), channel_id=1, source_target_pairs={{1,0},{2,3},{5,4},{6,7},{9,8},{10,11},{13,12},{14,15},{17,16},{18,... | collective-permute-start | bytes 1572872 | tf_op jit(solution)/shard_map/ppermute | solution.py:239
  262.1 16.3 %collective-permute-start.21 = (bf16[12,32,1024]{2,1,0:T(8,128)(2,1)S(1)}, bf16[12,32,1024]{2,1,0:T(8,128)(2,1)S(1)}, u32[]{:S(2)}, u32[]{:S(2)}) collective-permute-start(bf16[12,32,1024]{2,1,0:T(8,128)(2,1)S(1)} %pad_maximum_fusion.7), channel_id=1, source_target_pairs={{0,1},{3,2},{4,5},{7,6},{8,9},{11,10},{12,13},{15,14},{16,17},{19,... | collective-permute-start | bytes 2359304 | tf_op jit(solution)/shard_map/ppermute | solution.py:95
  266.8 19.5 %collective-permute-start.19 = (f32[8,32,1024]{2,1,0:T(8,128)S(1)}, f32[8,32,1024]{2,1,0:T(8,128)S(1)}, u32[]{:S(2)}, u32[]{:S(2)}) collective-permute-start(f32[8,32,1024]{2,1,0:T(8,128)S(1)} %convert_add_fusion.2), channel_id=1, source_target_pairs={{1,2},{2,1},{5,6},{6,5},{9,10},{10,9},{13,14},{14,13},{17,18},{18,... | collective-permute-start | bytes 3145736 | tf_op jit(solution)/shard_map/ppermute | solution.py:235
  267.6 3.7 %copy-start.10 = (f32[8,32,1024]{2,1,0:T(8,128)S(1)}, f32[8,32,1024]{2,1,0:T(8,128)}, u32[]{:S(2)}) copy-start(f32[8,32,1024]{2,1,0:T(8,128)} %shard_map.51) | copy-start | bytes 3145732
  267.6 3.8 %copy-start.18 = (f32[8,32,1024]{2,1,0:T(8,128)S(1)}, f32[8,32,1024]{2,1,0:T(8,128)}, u32[]{:S(2)}) copy-start(f32[8,32,1024]{2,1,0:T(8,128)} %copy-done.17) | copy-start | bytes 3145732
  271.4 16.2 %collective-permute-start.11 = (f32[4,32,1024]{2,1,0:T(8,128)S(1)}, f32[4,32,1024]{2,1,0:T(8,128)S(1)}, u32[]{:S(2)}, u32[]{:S(2)}) collective-permute-start(f32[4,32,1024]{2,1,0:T(8,128)S(1)} %slice_add_fusion.11), channel_id=1, source_target_pairs={{1,0},{2,3},{5,4},{6,7},{9,8},{10,11},{13,12},{14,15},{17,16},{18,... | collective-permute-start | bytes 1572872 | tf_op jit(solution)/shard_map/ppermute | solution.py:239
  278.5 17.0 %collective-permute-start.24 = (bf16[12,32,1024]{2,1,0:T(8,128)(2,1)S(1)}, bf16[12,32,1024]{2,1,0:T(8,128)(2,1)S(1)}, u32[]{:S(2)}, u32[]{:S(2)}) collective-permute-start(bf16[12,32,1024]{2,1,0:T(8,128)(2,1)S(1)} %pad_maximum_fusion.8), channel_id=1, source_target_pairs={{0,1},{3,2},{4,5},{7,6},{8,9},{11,10},{12,13},{15,14},{16,17},{19,... | collective-permute-start | bytes 2359304 | tf_op jit(solution)/shard_map/ppermute | solution.py:95
  286.2 4.8 %copy-start.9 = (f32[8,32,1024]{2,1,0:T(8,128)S(1)}, f32[8,32,1024]{2,1,0:T(8,128)}, u32[]{:S(2)}) copy-start(f32[8,32,1024]{2,1,0:T(8,128)} %shard_map.53) | copy-start | bytes 3145732
  286.2 7.2 %copy-start.14 = (f32[8,32,1024]{2,1,0:T(8,128)S(1)}, f32[8,32,1024]{2,1,0:T(8,128)}, u32[]{:S(2)}) copy-start(f32[8,32,1024]{2,1,0:T(8,128)} %shard_map.55) | copy-start | bytes 3145732
  286.3 9.4 %collective-permute-start.22 = (f32[8,32,1024]{2,1,0:T(8,128)S(1)}, f32[8,32,1024]{2,1,0:T(8,128)S(1)}, u32[]{:S(2)}, u32[]{:S(2)}) collective-permute-start(f32[8,32,1024]{2,1,0:T(8,128)S(1)} %convert_add_fusion.1), channel_id=1, source_target_pairs={{1,2},{2,1},{5,6},{6,5},{9,10},{10,9},{13,14},{14,13},{17,18},{18,... | collective-permute-start | bytes 3145736 | tf_op jit(solution)/shard_map/ppermute | solution.py:235
  292.1 19.5 %collective-permute-start.14 = (f32[4,32,1024]{2,1,0:T(8,128)S(1)}, f32[4,32,1024]{2,1,0:T(8,128)S(1)}, u32[]{:S(2)}, u32[]{:S(2)}) collective-permute-start(f32[4,32,1024]{2,1,0:T(8,128)S(1)} %slice_add_fusion.9), channel_id=1, source_target_pairs={{1,0},{2,3},{5,4},{6,7},{9,8},{10,11},{13,12},{14,15},{17,16},{18,... | collective-permute-start | bytes 1572872 | tf_op jit(solution)/shard_map/ppermute | solution.py:239
  293.5 23.7 %collective-permute-start.17 = (f32[4,32,1024]{2,1,0:T(8,128)S(1)}, f32[4,32,1024]{2,1,0:T(8,128)S(1)}, u32[]{:S(2)}, u32[]{:S(2)}) collective-permute-start(f32[4,32,1024]{2,1,0:T(8,128)S(1)} %slice_add_fusion.7), channel_id=1, source_target_pairs={{1,0},{2,3},{5,4},{6,7},{9,8},{10,11},{13,12},{14,15},{17,16},{18,... | collective-permute-start | bytes 1572872 | tf_op jit(solution)/shard_map/ppermute | solution.py:239
  295.7 27.7 %collective-permute-start.25 = (f32[8,32,1024]{2,1,0:T(8,128)S(1)}, f32[8,32,1024]{2,1,0:T(8,128)S(1)}, u32[]{:S(2)}, u32[]{:S(2)}) collective-permute-start(f32[8,32,1024]{2,1,0:T(8,128)S(1)} %convert_add_fusion), channel_id=1, source_target_pairs={{1,2},{2,1},{5,6},{6,5},{9,10},{10,9},{13,14},{14,13},{17,18},{18,... | collective-permute-start | bytes 3145736 | tf_op jit(solution)/shard_map/ppermute | solution.py:235
  315.2 5.4 %copy-start.16 = (f32[8,32,1024]{2,1,0:T(8,128)S(1)}, f32[8,32,1024]{2,1,0:T(8,128)}, u32[]{:S(2)}) copy-start(f32[8,32,1024]{2,1,0:T(8,128)} %shard_map.57) | copy-start | bytes 3145732
  315.2 6.8 %copy-start.15 = (f32[8,32,1024]{2,1,0:T(8,128)S(1)}, f32[8,32,1024]{2,1,0:T(8,128)}, u32[]{:S(2)}) copy-start(f32[8,32,1024]{2,1,0:T(8,128)} %shard_map.59) | copy-start | bytes 3145732
  320.7 21.0 %collective-permute-start.20 = (f32[4,32,1024]{2,1,0:T(8,128)S(1)}, f32[4,32,1024]{2,1,0:T(8,128)S(1)}, u32[]{:S(2)}, u32[]{:S(2)}) collective-permute-start(f32[4,32,1024]{2,1,0:T(8,128)S(1)} %slice_add_fusion.5), channel_id=1, source_target_pairs={{1,0},{2,3},{5,4},{6,7},{9,8},{10,11},{13,12},{14,15},{17,16},{18,... | collective-permute-start | bytes 1572872 | tf_op jit(solution)/shard_map/ppermute | solution.py:239
  322.1 25.2 %collective-permute-start.23 = (f32[4,32,1024]{2,1,0:T(8,128)S(1)}, f32[4,32,1024]{2,1,0:T(8,128)S(1)}, u32[]{:S(2)}, u32[]{:S(2)}) collective-permute-start(f32[4,32,1024]{2,1,0:T(8,128)S(1)} %slice_add_fusion.3), channel_id=1, source_target_pairs={{1,0},{2,3},{5,4},{6,7},{9,8},{10,11},{13,12},{14,15},{17,16},{18,... | collective-permute-start | bytes 1572872 | tf_op jit(solution)/shard_map/ppermute | solution.py:239
  323.5 29.4 %collective-permute-start.26 = (f32[4,32,1024]{2,1,0:T(8,128)S(1)}, f32[4,32,1024]{2,1,0:T(8,128)S(1)}, u32[]{:S(2)}, u32[]{:S(2)}) collective-permute-start(f32[4,32,1024]{2,1,0:T(8,128)S(1)} %slice_add_fusion.1), channel_id=1, source_target_pairs={{1,0},{2,3},{5,4},{6,7},{9,8},{10,11},{13,12},{14,15},{17,16},{18,... | collective-permute-start | bytes 1572872 | tf_op jit(solution)/shard_map/ppermute | solution.py:239
  349.7 3.2 copy-start.19
  (2 other events, 2.9 us)
